TPU v7x, 512 devices: a whole 4x4x16 slice. The times are simulated.
512 devices in a mesh: sec: 2 (over core), section: 4 (over z_hi), expert: 64 (over y, x, z_lo).
Axes of the slice: x: 4, y: 4, z: 16 (z_hi: 4, z_lo: 4; z = z_hi * 4 + z_lo), core: 2. Of those that a mesh axis runs over, the one named last changes fastest.
Arguments:
- tokens: bfloat16 [8192, 2048], P('expert', ('sec', 'section')), may hold values from -6 to 6
- cotangent: bfloat16 [8192, 2048], P('expert', ('sec', 'section')), may hold values from -6 to 6
- expert_ids: int32 [8192, 2], P('expert'), may hold values from 0 to 63, all different within a row; in each aligned block of 128 rows (0 to 127, 128 to 255, ...) at most 6 rows name the same one
- gate_values: float32 [8192, 2], P('expert'), may hold values from 0.2 to 1
- expand_weight: bfloat16 [64, 2048, 4096], P('expert', None, ('sec', 'section')), may hold values from -0.125 to 0.125
- contract_weight: bfloat16 [64, 4096, 2048], P('expert', ('sec', 'section')), may hold values from -0.09375 to 0.09375
Outputs:
- combined: bfloat16 [8192, 2048], P('expert', ('sec', 'section'))
- input_grad: bfloat16 [8192, 2048], P('expert', ('sec', 'section'))
- gate_grad: float32 [8192, 2], P('expert')
Inputs may be any that keep to these rules, and one draw needn't show every extreme that they name: `expert_ids`: the two ids of a token differ. Among the 128 tokens of one index of expert, no expert is named by more than 6 of them, a bound that some block reaches.
All inputs are finite; a program needn't handle non-finite values.
Results may differ from a plain program's by a relative error of at most 0.015.
Values may be sent and summed in bfloat16 or wider, within the bound.
No kernel may reach another device: no remote copies, remote signals or barrier semaphores. Data moves between devices by JAX's collectives and lax.ppermute only.
A program may use at most 64 MiB of HBM per device.

v0:
```python
import math

import jax
import jax.numpy as jnp
from jax import lax
from jax.sharding import PartitionSpec as P

gelu_coef = math.sqrt(2.0 / math.pi)
gelu_cubic = 0.044715


def gelu_parts(hidden):
    inner_arg = gelu_coef * (hidden + gelu_cubic * hidden * hidden * hidden)
    tanh_value = jnp.tanh(inner_arg)
    activation = 0.5 * hidden * (1.0 + tanh_value)
    derivative = 0.5 * (1.0 + tanh_value) + 0.5 * hidden * (
        1.0 - tanh_value * tanh_value
    ) * gelu_coef * (1.0 + 3.0 * gelu_cubic * hidden * hidden)
    return (activation, derivative)


def slot_positions(expert_ids, capacity, experts):
    flat_ids = expert_ids.reshape(-1)
    one_hot = (flat_ids[:, None] == jnp.arange(experts, dtype=jnp.int32)[None, :]).astype(jnp.int32)
    earlier = jnp.sum((jnp.cumsum(one_hot, axis=0) - one_hot) * one_hot, axis=1)
    return flat_ids * capacity + earlier


def transposed_product(left, right):
    return lax.dot_general(
        left, right, (((1,), (1,)), ((), ())), preferred_element_type=jnp.float32
    )


def per_device(tokens, cotangent, expert_ids, gate_values, expand_weight, contract_weight):
    block_index = lax.axis_index("sec") * lax.axis_size("section") + lax.axis_index("section")
    tok_rows, width_share = tokens.shape
    experts = lax.axis_size("expert")
    capacity = 3 * tok_rows // experts
    slot_count = experts * capacity
    expand_local = expand_weight[0]
    contract_local = contract_weight[0]
    full_width = contract_local.shape[1]
    positions = slot_positions(expert_ids, capacity, experts)
    placement_matrix = (
        positions[:, None] == jnp.arange(slot_count, dtype=jnp.int32)[None, :]
    ).astype(jnp.bfloat16)
    scaled_grad = (gate_values[:, :, None] * cotangent[:, None, :].astype(jnp.float32)).astype(
        jnp.bfloat16
    )

    def to_slots(pairs):
        return jnp.dot(placement_matrix.T, pairs, preferred_element_type=jnp.float32).astype(
            jnp.bfloat16
        )

    whole_tokens, whole_grad = (
        lax.all_gather(tokens, ("sec", "section"), axis=1, tiled=True),
        lax.all_gather(scaled_grad, ("sec", "section"), axis=2, tiled=True),
    )
    pair_tokens = jnp.broadcast_to(whole_tokens[:, None, :], (tok_rows, 2, full_width)).reshape(
        2 * tok_rows, full_width
    )
    send_x = to_slots(pair_tokens).reshape(experts, capacity, full_width)
    send_g = to_slots(whole_grad.reshape(2 * tok_rows, full_width)).reshape(
        experts, capacity, full_width
    )
    recv_x, recv_g = (
        lax.all_to_all(send_x, "expert", split_axis=0, concat_axis=0, tiled=True),
        lax.all_to_all(send_g, "expert", split_axis=0, concat_axis=0, tiled=True),
    )
    hidden = jnp.dot(
        recv_x.reshape(slot_count, full_width), expand_local, preferred_element_type=jnp.float32
    )
    grad_activation = transposed_product(recv_g.reshape(slot_count, full_width), contract_local)
    activation, derivative = gelu_parts(hidden)
    activation = activation.astype(jnp.bfloat16)
    grad_hidden = (grad_activation * derivative).astype(jnp.bfloat16)
    out_part = jnp.dot(activation, contract_local, preferred_element_type=jnp.float32).astype(
        jnp.bfloat16
    )
    back_part = transposed_product(grad_hidden, expand_local).astype(jnp.bfloat16)
    out_sum, back_sum = (
        lax.psum(out_part, ("sec", "section")).astype(jnp.float32),
        lax.psum(back_part, ("sec", "section")).astype(jnp.float32),
    )
    out_rows = out_sum.astype(jnp.bfloat16).reshape(experts, capacity, full_width)
    back_rows = back_sum.astype(jnp.bfloat16).reshape(experts, capacity, full_width)
    returned_out, returned_back = (
        lax.all_to_all(out_rows, "expert", split_axis=0, concat_axis=0, tiled=True),
        lax.all_to_all(back_rows, "expert", split_axis=0, concat_axis=0, tiled=True),
    )
    returned_out = lax.dynamic_slice_in_dim(returned_out, block_index * width_share, width_share, 2)
    returned_back = lax.dynamic_slice_in_dim(
        returned_back, block_index * width_share, width_share, 2
    )
    out_pairs = jnp.dot(
        placement_matrix,
        returned_out.reshape(slot_count, width_share),
        preferred_element_type=jnp.float32,
    ).reshape(tok_rows, 2, width_share)
    back_pairs = jnp.dot(
        placement_matrix,
        returned_back.reshape(slot_count, width_share),
        preferred_element_type=jnp.float32,
    ).reshape(tok_rows, 2, width_share)
    combined = jnp.sum(gate_values[:, :, None] * out_pairs, axis=1).astype(jnp.bfloat16)
    partial_dots = jnp.sum(cotangent[:, None, :].astype(jnp.float32) * out_pairs, axis=2)
    gate_grad = lax.psum(partial_dots, ("sec", "section"))
    input_grad = (back_pairs[:, 0, :] + back_pairs[:, 1, :]).astype(jnp.bfloat16)
    return (combined, input_grad, gate_grad)


def solution(mesh):
    return jax.shard_map(
        per_device,
        mesh=mesh,
        in_specs=(
            P("expert", ("sec", "section")),
            P("expert", ("sec", "section")),
            P("expert", None),
            P("expert", None),
            P("expert", None, ("sec", "section")),
            P("expert", ("sec", "section"), None),
        ),
        out_specs=(
            P("expert", ("sec", "section")),
            P("expert", ("sec", "section")),
            P("expert", None),
        ),
        check_vma=False,
    )
```

profile of v0, /device:TPU:1, one launch (start us, length us, event | category | flops | bytes accessed | tf_op | source)
XLA Modules:
  0.0 729.8 jit_solution(12171492851561953252)
XLA Ops:
  7.2 0.0 copy-start
  7.2 0.9 copy.16
  8.1 0.1 eq.69
  8.3 0.1 eq.65
  8.4 0.6 reduce-window.6
  9.0 0.2 slice_reduce_fusion
  9.3 0.1 fusion.50
  9.4 49.3 %all_gather.6 = bf16[128,2048]{1,0:T(8,128)(2,1)S(1)} all-gather(bf16[128,256]{1,0:T(8,128)(2,1)} %param.6), channel_id=1, replica_groups=mesh['sec'=2,'section'=4,'expert'=64] {'sec','section'}, dimensions={1}, use_global_device_ids=true | all-gather | bytes 589824 | tf_op jit(solution)/shard_map/all_gather | solution.py:58
  58.7 1.6 broadcast_in_dim.2
  60.3 1.5 reshape.109
  61.8 1.8 convolution_convert_fusion.3
  63.6 3.7 reshape.110
  67.3 0.0 copy-start.1
  67.3 0.0 copy-start.3
  67.3 9.9 %all-to-all-start = ((bf16[64,6,2048]{2,1,0:T(8,128)(2,1)}), bf16[64,6,2048]{2,1,0:T(8,128)(2,1)}, u32[]{:S(2)}, u32[]{:S(2)}) async-start(bf16[64,6,2048]{2,1,0:T(8,128)(2,1)} %reshape.110), calls=%async_computation | async-start | bytes 4194304 | tf_op jit(solution)/shard_map/all_to_all | solution.py:69
  77.3 0.0 all-gather.2.cloned.1.call-start
  77.3 0.0 copy-done.1
  77.4 0.0 copy-done.3
  77.4 0.7 multiply_convert_fusion.2
  78.1 0.0 all-gather.2.cloned.1.call-update
  78.1 50.1 %all-gather.2.cloned.1.call-done = bf16[128,2,2048]{2,0,1:T(8,128)(2,1)} async-done(((bf16[128,2,256]{2,0,1:T(8,128)(2,1)}), bf16[128,2,2048]{2,0,1:T(8,128)(2,1)}) %all-gather.2.cloned.1.call-update) | async-done | bytes 1048592 | tf_op jit(solution)/shard_map/all_gather | solution.py:59
  128.2 3.3 copy.20
  131.5 1.5 reshape.114
  133.0 1.8 convolution_convert_fusion.1
  134.8 3.7 reshape.115
  138.6 6.6 all-to-all-done
  145.1 10.7 %all-to-all-start.2 = ((bf16[64,6,2048]{2,1,0:T(8,128)(2,1)}), bf16[64,6,2048]{2,1,0:T(8,128)(2,1)}, u32[]{:S(2)}, u32[]{:S(2)}) async-start(bf16[64,6,2048]{2,1,0:T(8,128)(2,1)} %reshape.115), calls=%async_computation.2 | async-start | bytes 4194304 | tf_op jit(solution)/shard_map/all_to_all | solution.py:70
  155.8 0.0 all-reduce.3.cloned.1.call-start
  155.9 3.7 reshape.111
  159.6 3.0 fusion.4
  162.6 0.0 copy-done
  162.6 2.2 convolution_convert_fusion.2
  164.8 3.7 reshape.112
  168.5 38.2 %all-to-all-done.2 = bf16[64,6,2048]{2,1,0:T(8,128)(2,1)} async-done(((bf16[64,6,2048]{2,1,0:T(8,128)(2,1)}), bf16[64,6,2048]{2,1,0:T(8,128)(2,1)}, u32[]{:S(2)}, u32[]{:S(2)}) %all-to-all-start.2) | async-done | bytes 1572896 | tf_op jit(solution)/shard_map/all_to_all | solution.py:70
  206.7 3.7 reshape.116
  210.4 5.4 convolution_convert_fusion
  215.8 3.7 reshape.117
  219.5 0.0 all-reduce.3.cloned.1.call-update
  219.6 361.5 %all-reduce.3.cloned.1.call-done = (bf16[64,6,2048]{2,1,0:T(8,128)(2,1)}, bf16[64,6,2048]{2,1,0:T(8,128)(2,1)}) async-done(((bf16[64,6,2048]{2,1,0:T(8,128)(2,1)}, bf16[64,6,2048]{2,1,0:T(8,128)(2,1)}), (bf16[64,6,2048]{2,1,0:T(8,128)(2,1)}, bf16[64,6,2048]{2,1,0:T(8,128)(2,1)})) %all-reduce.3.cloned.1.call-update) | async-done | bytes 3145744 | tf_op jit(solution)/shard_map/psum | solution.py:84
  581.1 58.7 %all_to_all.20 = bf16[64,6,2048]{2,1,0:T(8,128)(2,1)} all-to-all(bf16[64,6,2048]{2,1,0:T(8,128)(2,1)} %get-tuple-element.5), channel_id=1, replica_groups=mesh['sec'=2,'section'=4,'expert'=64] {'expert'}, dimensions={0} | all-to-all | bytes 3145728 | tf_op jit(solution)/shard_map/all_to_all | solution.py:90
  639.8 0.0 copy-start.2
  639.8 5.7 all-to-all-start.3
  645.5 0.1 reduce_sum.30
  645.7 0.1 copy.19
  645.7 0.0 copy-done.2
  645.7 50.0 %all-to-all-done.3 = bf16[64,6,2048]{2,1,0:T(8,128)(2,1)} async-done(((bf16[64,6,2048]{2,1,0:T(8,128)(2,1)}), bf16[64,6,2048]{2,1,0:T(8,128)(2,1)}, u32[]{:S(2)}, u32[]{:S(2)}) %all-to-all-start.3) | async-done | bytes 1572896 | tf_op jit(solution)/shard_map/all_to_all | solution.py:91
  695.8 1.1 constant_dynamic-slice_fusion
  696.8 0.1 reshape.120
  696.9 0.3 fusion.38
  697.2 0.6 fusion.47
  697.8 0.1 reshape.119
  697.9 1.0 multiply_reduce_fusion
  698.9 24.0 %psum.23 = f32[128,2]{0,1:T(2,128)} all-reduce(f32[128,2]{0,1:T(2,128)S(1)} %get-tuple-element.3), channel_id=1, replica_groups=mesh['sec'=2,'section'=4,'expert'=64] {'sec','section'}, use_global_device_ids=true, to_apply=%region_7.8 | all-reduce | flops 256 | bytes 2048 | tf_op jit(solution)/shard_map/psum | solution.py:109
  (6 shorter events, 0.1 us)
Async XLA Ops:
  7.2 155.5 %copy-start = (bf16[1,512,2048]{2,1,0:T(8,128)(2,1)S(1)}, bf16[1,512,2048]{2,1,0:T(8,128)(2,1)}, u32[]{:S(2)}) copy-start(bf16[1,512,2048]{2,1,0:T(8,128)(2,1)} %param.11) | copy-start | bytes 6291460
  67.3 10.0 %copy-start.1 = (bf16[128,256]{1,0:T(8,128)(2,1)S(1)}, bf16[128,256]{1,0:T(8,128)(2,1)}, u32[]{:S(2)}) copy-start(bf16[128,256]{1,0:T(8,128)(2,1)} %param.7) | copy-start | bytes 196612
  67.3 10.0 %copy-start.3 = (f32[128,2]{0,1:T(2,128)S(1)}, f32[128,2]{0,1:T(2,128)}, u32[]{:S(2)}) copy-start(f32[128,2]{0,1:T(2,128)} %param.9) | copy-start | bytes 3076
  67.3 77.8 %all-to-all-start = ((bf16[64,6,2048]{2,1,0:T(8,128)(2,1)}), bf16[64,6,2048]{2,1,0:T(8,128)(2,1)}, u32[]{:S(2)}, u32[]{:S(2)}) async-start(bf16[64,6,2048]{2,1,0:T(8,128)(2,1)} %reshape.110), calls=%async_computation | async-start | bytes 4194304 | tf_op jit(solution)/shard_map/all_to_all | solution.py:69
  77.3 50.9 %all-gather.2.cloned.1.call-start = ((), (), s32[]{:S(2)}) async-start(), calls=%async_computation.4 | async-start | bytes 1179648 | tf_op jit(solution)/shard_map/all_gather | solution.py:59
  145.1 61.6 %all-to-all-start.2 = ((bf16[64,6,2048]{2,1,0:T(8,128)(2,1)}), bf16[64,6,2048]{2,1,0:T(8,128)(2,1)}, u32[]{:S(2)}, u32[]{:S(2)}) async-start(bf16[64,6,2048]{2,1,0:T(8,128)(2,1)} %reshape.115), calls=%async_computation.2 | async-start | bytes 4194304 | tf_op jit(solution)/shard_map/all_to_all | solution.py:70
  155.8 425.3 %all-reduce.3.cloned.1.call-start = ((), (), s32[]{:S(2)}) async-start(), calls=%async_computation.5 | async-start | bytes 8388608 | tf_op jit(solution)/shard_map/psum | solution.py:84
  639.8 5.9 copy-start.2
  639.8 56.0 %all-to-all-start.3 = ((bf16[64,6,2048]{2,1,0:T(8,128)(2,1)}), bf16[64,6,2048]{2,1,0:T(8,128)(2,1)}, u32[]{:S(2)}, u32[]{:S(2)}) async-start(bf16[64,6,2048]{2,1,0:T(8,128)(2,1)} %get-tuple-element.6), calls=%async_computation.3 | async-start | bytes 4194304 | tf_op jit(solution)/shard_map/all_to_all | solution.py:91
Sparse Core Ops, SparseCore 0:
  80.2 47.9 all-gather.1
  219.7 361.3 all-reduce.2
where the time goes:
time: 731 us; the launch traced here: 730 us
  waiting for transfers between devices  506 us (69%)
  blocking collectives  132 us (18%)
  local copies, waits for them, and re-layouts  32.9 us (5%)
  starting transfers between devices  26.4 us (4%)
  matrix products  15.6 us (2%)
  between operations  14.2 us (2%)
    psum x1, waiting for transfers between devices, per_device(): lax.psum(out_part, ('sec', 'section')).astype(jnp.float32)  362 us
    all_to_all x1, blocking collectives, per_device(): lax.all_to_all(out_rows, 'expert', split_axis=0, concat_axis=0, tiled=True)  58.7 us
    all_gather x1, waiting for transfers between devices, per_device(): lax.all_gather(scaled_grad, ('sec', 'section'), axis=2, tiled=True)  50.1 us
    all_to_all x1, waiting for transfers between devices, per_device(): lax.all_to_all(back_rows, 'expert', split_axis=0, concat_axis=0, tiled=True)  50 us
    all_gather x1, blocking collectives, per_device(): lax.all_gather(tokens, ('sec', 'section'), axis=1, tiled=True)  49.3 us
    all_to_all x1, waiting for transfers between devices, per_device(): lax.all_to_all(send_g, 'expert', split_axis=0, concat_axis=0, tiled=True)  38.2 us
    psum x1, blocking collectives, per_device(): gate_grad = lax.psum(partial_dots, ('sec', 'section'))  24 us
  transfers between devices with their start and end apart: 5, of which 5 were waited for; matrix products, arithmetic and copies ran while one was open for 3% of the time, Pallas kernels for 0%

commit v1 on v0

v1 whole, which is shorter than its diff:
```python
import math

import jax
import jax.numpy as jnp
from jax import lax
from jax.sharding import PartitionSpec as P

gelu_coef = math.sqrt(2.0 / math.pi)
gelu_cubic = 0.044715


def gelu_parts(hidden):
    inner_arg = gelu_coef * (hidden + gelu_cubic * hidden * hidden * hidden)
    tanh_value = jnp.tanh(inner_arg)
    activation = 0.5 * hidden * (1.0 + tanh_value)
    derivative = 0.5 * (1.0 + tanh_value) + 0.5 * hidden * (
        1.0 - tanh_value * tanh_value
    ) * gelu_coef * (1.0 + 3.0 * gelu_cubic * hidden * hidden)
    return (activation, derivative)


def slot_positions(expert_ids, capacity, experts):
    flat_ids = expert_ids.reshape(-1)
    one_hot = (flat_ids[:, None] == jnp.arange(experts, dtype=jnp.int32)[None, :]).astype(jnp.int32)
    earlier = jnp.sum((jnp.cumsum(one_hot, axis=0) - one_hot) * one_hot, axis=1)
    return flat_ids * capacity + earlier


def transposed_product(left, right):
    return lax.dot_general(
        left, right, (((1,), (1,)), ((), ())), preferred_element_type=jnp.float32
    )


BLOCK_AXES = ("sec", "section")


def per_device(tokens, cotangent, expert_ids, gate_values, expand_weight, contract_weight):
    tok_rows, width_share = tokens.shape
    experts = lax.axis_size("expert")
    capacity = 3 * tok_rows // experts
    slot_count = experts * capacity
    expand_local = expand_weight[0]
    contract_local = contract_weight[0]
    full_width = contract_local.shape[1]
    positions = slot_positions(expert_ids, capacity, experts)
    placement_matrix = (
        positions[:, None] == jnp.arange(slot_count, dtype=jnp.int32)[None, :]
    ).astype(jnp.bfloat16)

    def to_slots(pairs):
        return jnp.dot(placement_matrix.T, pairs, preferred_element_type=jnp.float32).astype(
            jnp.bfloat16
        )

    whole_tokens = lax.all_gather(tokens, BLOCK_AXES, axis=1, tiled=True)
    whole_cot = lax.all_gather(cotangent, BLOCK_AXES, axis=1, tiled=True)
    whole_grad = (gate_values[:, :, None] * whole_cot[:, None, :].astype(jnp.float32)).astype(
        jnp.bfloat16
    )
    pair_tokens = jnp.broadcast_to(whole_tokens[:, None, :], (tok_rows, 2, full_width)).reshape(
        2 * tok_rows, full_width
    )
    send_x = to_slots(pair_tokens).reshape(experts, capacity, full_width)
    send_g = to_slots(whole_grad.reshape(2 * tok_rows, full_width)).reshape(
        experts, capacity, full_width
    )
    recv_x = lax.all_to_all(send_x, "expert", split_axis=0, concat_axis=0, tiled=True)
    hidden = jnp.dot(
        recv_x.reshape(slot_count, full_width), expand_local, preferred_element_type=jnp.float32
    )
    activation, derivative = gelu_parts(hidden)
    activation = activation.astype(jnp.bfloat16)
    out_part = jnp.dot(activation, contract_local, preferred_element_type=jnp.float32).astype(
        jnp.bfloat16
    )
    out_rows = lax.psum_scatter(out_part, BLOCK_AXES, scatter_dimension=1, tiled=True)
    returned_out = lax.all_to_all(
        out_rows.reshape(experts, capacity, width_share), "expert", split_axis=0, concat_axis=0,
        tiled=True,
    )

    recv_g = lax.all_to_all(send_g, "expert", split_axis=0, concat_axis=0, tiled=True)
    grad_activation = transposed_product(recv_g.reshape(slot_count, full_width), contract_local)
    grad_hidden = (grad_activation * derivative).astype(jnp.bfloat16)
    back_part = transposed_product(grad_hidden, expand_local).astype(jnp.bfloat16)
    back_rows = lax.psum_scatter(back_part, BLOCK_AXES, scatter_dimension=1, tiled=True)
    returned_back = lax.all_to_all(
        back_rows.reshape(experts, capacity, width_share), "expert", split_axis=0, concat_axis=0,
        tiled=True,
    )

    out_pairs = jnp.dot(
        placement_matrix,
        returned_out.reshape(slot_count, width_share),
        preferred_element_type=jnp.float32,
    ).reshape(tok_rows, 2, width_share)
    combined = jnp.sum(gate_values[:, :, None] * out_pairs, axis=1).astype(jnp.bfloat16)
    partial_dots = jnp.sum(cotangent[:, None, :].astype(jnp.float32) * out_pairs, axis=2)
    gate_grad = lax.psum(partial_dots, BLOCK_AXES)
    back_pairs = jnp.dot(
        placement_matrix,
        returned_back.reshape(slot_count, width_share),
        preferred_element_type=jnp.float32,
    ).reshape(tok_rows, 2, width_share)
    input_grad = (back_pairs[:, 0, :] + back_pairs[:, 1, :]).astype(jnp.bfloat16)
    return (combined, input_grad, gate_grad)


def solution(mesh):
    return jax.shard_map(
        per_device,
        mesh=mesh,
        in_specs=(
            P("expert", BLOCK_AXES),
            P("expert", BLOCK_AXES),
            P("expert", None),
            P("expert", None),
            P("expert", None, BLOCK_AXES),
            P("expert", BLOCK_AXES, None),
        ),
        out_specs=(
            P("expert", BLOCK_AXES),
            P("expert", BLOCK_AXES),
            P("expert", None),
        ),
        check_vma=False,
    )
```

time: 731 us -> 470 us (0.64)
  waiting for transfers between devices: 506 us -> 205 us
  starting transfers between devices: 26.4 us -> 54.5 us
  blocking collectives: 132 us -> 144 us
    psum x1 -> x0, waiting for transfers between devices: 362 us -> none  [per_device(): lax.psum(out_part, ('sec', 'section')).astype(jnp.float32)]
    reduce_scatter x0 -> x2, waiting for transfers between devices: none -> 153 us  [the longest x1 77.1 us: per_device(): lax.psum_scatter(back_part, BLOCK_AXES, scatter_dimension=1, tiled=True)]
    all_gather x1 -> x2, blocking collectives: 49.3 us -> 117 us  [the longest x1 67.9 us: per_device(): whole_cot = lax.all_gather(cotangent, BLOCK_AXES, axis=1, tiled=True)]
    all_to_all x1 -> x0, blocking collectives: 58.7 us -> none  [per_device(): lax.all_to_all(out_rows, 'expert', split_axis=0, concat_axis=0, tiled=True)]
    all_gather x1 -> x0, waiting for transfers between devices: 50.1 us -> none  [per_device(): lax.all_gather(scaled_grad, ('sec', 'section'), axis=2, tiled=True)]
    all_to_all x1 -> x2, waiting for transfers between devices: 50 us -> 9.35 us  [the longest x1 9.35 us: per_device(): lax.all_to_all(out_rows.reshape(experts, capacity, width_share), 'expert'...]
    all_to_all x1 -> x2, starting transfers between devices: 5.69 us -> 20.2 us  [the longest x1 11.3 us: per_device(): lax.all_to_all(back_rows.reshape(experts, capacity, width_share), 'expert...]
    all_to_all x1, starting transfers between devices: 10.7 us -> 24.3 us  [per_device(): lax.all_to_all(send_g, 'expert', split_axis=0, concat_axis=0, tiled=True)]
  transfers between devices with their start and end apart: 5 -> 6, of which waited for: 5 -> 4; matrix products, arithmetic and copies ran while one was open for 3% -> 6% of each run, Pallas kernels for 0% -> 0%
where the time goes in v1:
time: 470 us; the launch traced here: 469 us
  waiting for transfers between devices  205 us (44%)
  blocking collectives  144 us (31%)
  starting transfers between devices  54.5 us (12%)
  local copies, waits for them, and re-layouts  29.4 us (6%)
  matrix products  19.5 us (4%)
  between operations  14.2 us (3%)
    reduce_scatter x1, waiting for transfers between devices, per_device(): lax.psum_scatter(back_part, BLOCK_AXES, scatter_dimension=1, tiled=True)  77.1 us
    reduce_scatter x1, waiting for transfers between devices, per_device(): lax.psum_scatter(out_part, BLOCK_AXES, scatter_dimension=1, tiled=True)  76.2 us
    all_gather x1, blocking collectives, per_device(): whole_cot = lax.all_gather(cotangent, BLOCK_AXES, axis=1, tiled=True)  67.9 us
    all_gather x1, blocking collectives, per_device(): whole_tokens = lax.all_gather(tokens, BLOCK_AXES, axis=1, tiled=True)  49.3 us
    all_to_all x1, waiting for transfers between devices, per_device(): lax.all_to_all(send_g, 'expert', split_axis=0, concat_axis=0, tiled=True)  42.8 us
    psum x1, blocking collectives, per_device(): gate_grad = lax.psum(partial_dots, BLOCK_AXES)  26.8 us
    all_to_all x1, starting transfers between devices, per_device(): lax.all_to_all(send_g, 'expert', split_axis=0, concat_axis=0, tiled=True)  24.3 us
    all_to_all x1, starting transfers between devices, per_device(): lax.all_to_all(back_rows.reshape(experts, capacity, width_share), 'expert...  11.3 us
  transfers between devices with their start and end apart: 6, of which 4 were waited for; matrix products, arithmetic and copies ran while one was open for 6% of the time, Pallas kernels for 0%

profile of v1, /device:TPU:1, one launch (start us, length us, event | category | flops | bytes accessed | tf_op | source)
XLA Modules:
  0.0 468.5 jit_solution(1711642674980327594)
XLA Ops:
  7.2 0.0 copy-start
  7.2 0.9 copy.16
  8.1 0.1 eq.69
  8.3 0.1 eq.65
  8.4 0.6 reduce-window.6
  9.0 0.2 slice_reduce_fusion
  9.3 0.1 fusion.51
  9.4 49.3 %all_gather.6 = bf16[128,2048]{1,0:T(8,128)(2,1)S(1)} all-gather(bf16[128,256]{1,0:T(8,128)(2,1)} %param.6), channel_id=1, replica_groups=mesh['sec'=2,'section'=4,'expert'=64] {'sec','section'}, dimensions={1}, use_global_device_ids=true | all-gather | bytes 589824 | tf_op jit(solution)/shard_map/all_gather | solution.py:56
  58.7 1.6 broadcast_in_dim.2
  60.3 1.5 reshape.111
  61.8 1.8 convolution_convert_fusion.3
  63.6 3.7 reshape.112
  67.3 0.0 copy-start.1
  67.3 9.9 %all-to-all-start = ((bf16[64,6,2048]{2,1,0:T(8,128)(2,1)}), bf16[64,6,2048]{2,1,0:T(8,128)(2,1)}, u32[]{:S(2)}, u32[]{:S(2)}) async-start(bf16[64,6,2048]{2,1,0:T(8,128)(2,1)} %reshape.112), calls=%async_computation | async-start | bytes 4194304 | tf_op jit(solution)/shard_map/all_to_all | solution.py:68
  77.3 0.0 copy-done.1
  77.3 67.9 %all_gather.7 = bf16[128,2048]{1,0:T(8,128)(2,1)S(1)} all-gather(bf16[128,256]{1,0:T(8,128)(2,1)S(1)} %copy-done.1), channel_id=1, replica_groups=mesh['sec'=2,'section'=4,'expert'=64] {'sec','section'}, dimensions={1}, use_global_device_ids=true | all-gather | bytes 589824 | tf_op jit(solution)/shard_map/all_gather | solution.py:57
  145.2 2.4 mul.117
  147.6 0.0 copy-start.3
  147.6 3.7 mul.118
  151.3 0.0 copy-done.3
  151.3 0.1 copy.20
  151.4 0.1 mul.115
  151.6 3.4 convolution_convert_fusion.1
  155.0 3.7 reshape.116
  158.7 0.0 all-to-all-done
  158.7 24.3 %all-to-all-start.2 = ((bf16[64,6,2048]{2,1,0:T(8,128)(2,1)}), bf16[64,6,2048]{2,1,0:T(8,128)(2,1)}, u32[]{:S(2)}, u32[]{:S(2)}) async-start(bf16[64,6,2048]{2,1,0:T(8,128)(2,1)} %reshape.116), calls=%async_computation.3 | async-start | bytes 4194304 | tf_op jit(solution)/shard_map/all_to_all | solution.py:83
  183.0 0.0 reduce-scatter.5.cloned.1.call-start
  183.1 3.7 reshape.113
  186.8 3.9 fusion.4
  190.7 42.8 %all-to-all-done.2 = bf16[64,6,2048]{2,1,0:T(8,128)(2,1)} async-done(((bf16[64,6,2048]{2,1,0:T(8,128)(2,1)}), bf16[64,6,2048]{2,1,0:T(8,128)(2,1)}, u32[]{:S(2)}, u32[]{:S(2)}) %all-to-all-start.2) | async-done | bytes 1572896 | tf_op jit(solution)/shard_map/all_to_all | solution.py:83
  233.5 3.7 reshape.117
  237.2 0.0 copy-done
  237.2 5.7 %convolution_convert_fusion = bf16[384,2048]{1,0:T(8,128)(2,1)} fusion(bf16[1,2048,512]{2,1,0:T(8,128)(2,1)} %param.10, bf16[384,2048]{1,0:T(8,128)(2,1)} %reshape.117, bf16[1,512,2048]{2,1,0:T(8,128)(2,1)S(1)} %copy-done, f32[384,512]{1,0:T(8,128)} %fusion.4), kind=kOutput, calls=%fused_computation | convolution fusion | flops 1615134720 | bytes 8126464 | tf_op jit(solution)/shard_map/dot_general | solution.py:30
  242.9 0.0 reduce-scatter.5.cloned.1.call-update
  242.9 0.0 reduce-scatter.3.cloned.1.call-start
  243.0 3.4 convolution_convert_fusion.2
  246.3 0.0 copy-start.2
  246.3 0.0 reduce-scatter.3.cloned.1.call-update
  246.4 77.1 %reduce-scatter.5.cloned.1.call-done = bf16[384,256]{1,0:T(8,128)(2,1)} async-done(((bf16[384,2048]{1,0:T(8,128)(2,1)}), bf16[384,256]{1,0:T(8,128)(2,1)}) %reduce-scatter.5.cloned.1.call-update) | async-done | bytes 196624 | tf_op jit(solution)/shard_map/reduce_scatter | solution.py:87
  323.5 1.7 reshape.118
  325.2 11.3 %all-to-all-start.3 = ((bf16[64,6,256]{2,1,0:T(8,128)(2,1)}), bf16[64,6,256]{2,1,0:T(8,128)(2,1)S(1)}, u32[]{:S(2)}, u32[]{:S(2)}) async-start(bf16[64,6,256]{2,1,0:T(8,128)(2,1)} %reshape.118), calls=%async_computation.5 | async-start | bytes 524288 | tf_op jit(solution)/shard_map/all_to_all | solution.py:88
  336.4 76.2 %reduce-scatter.3.cloned.1.call-done = bf16[384,256]{1,0:T(8,128)(2,1)} async-done(((bf16[384,2048]{1,0:T(8,128)(2,1)}), bf16[384,256]{1,0:T(8,128)(2,1)}) %reduce-scatter.3.cloned.1.call-update) | async-done | bytes 196624 | tf_op jit(solution)/shard_map/reduce_scatter | solution.py:77
  412.6 1.7 reshape.114
  414.3 0.0 all-to-all-done.3
  414.3 9.0 %all-to-all-start.1 = ((bf16[64,6,256]{2,1,0:T(8,128)(2,1)}), bf16[64,6,256]{2,1,0:T(8,128)(2,1)S(1)}, u32[]{:S(2)}, u32[]{:S(2)}) async-start(bf16[64,6,256]{2,1,0:T(8,128)(2,1)} %reshape.114), calls=%async_computation.2 | async-start | bytes 524288 | tf_op jit(solution)/shard_map/all_to_all | solution.py:78
  423.2 0.1 reduce_sum.30
  423.4 0.1 copy.19
  423.5 0.0 copy-done.2
  423.5 0.1 reshape.121
  423.6 0.3 fusion.39
  423.8 0.6 fusion.48
  424.5 9.4 %all-to-all-done.1 = bf16[64,6,256]{2,1,0:T(8,128)(2,1)S(1)} async-done(((bf16[64,6,256]{2,1,0:T(8,128)(2,1)}), bf16[64,6,256]{2,1,0:T(8,128)(2,1)S(1)}, u32[]{:S(2)}, u32[]{:S(2)}) %all-to-all-start.1) | async-done | bytes 196640 | tf_op jit(solution)/shard_map/all_to_all | solution.py:78
  433.9 0.1 reshape.120
  433.9 1.0 multiply_reduce_fusion
  434.9 26.8 %psum.7 = f32[128,2]{0,1:T(2,128)} all-reduce(f32[128,2]{0,1:T(2,128)S(1)} %get-tuple-element.3), channel_id=1, replica_groups=mesh['sec'=2,'section'=4,'expert'=64] {'sec','section'}, use_global_device_ids=true, to_apply=%region_7.8 | all-reduce | flops 256 | bytes 2048 | tf_op jit(solution)/shard_map/psum | solution.py:100
  (6 shorter events, 0.1 us)
Async XLA Ops:
  7.2 230.1 %copy-start = (bf16[1,512,2048]{2,1,0:T(8,128)(2,1)S(1)}, bf16[1,512,2048]{2,1,0:T(8,128)(2,1)}, u32[]{:S(2)}) copy-start(bf16[1,512,2048]{2,1,0:T(8,128)(2,1)} %param.11) | copy-start | bytes 6291460
  67.3 10.0 %copy-start.1 = (bf16[128,256]{1,0:T(8,128)(2,1)S(1)}, bf16[128,256]{1,0:T(8,128)(2,1)}, u32[]{:S(2)}) copy-start(bf16[128,256]{1,0:T(8,128)(2,1)} %param.7) | copy-start | bytes 196612
  67.3 91.4 %all-to-all-start = ((bf16[64,6,2048]{2,1,0:T(8,128)(2,1)}), bf16[64,6,2048]{2,1,0:T(8,128)(2,1)}, u32[]{:S(2)}, u32[]{:S(2)}) async-start(bf16[64,6,2048]{2,1,0:T(8,128)(2,1)} %reshape.112), calls=%async_computation | async-start | bytes 4194304 | tf_op jit(solution)/shard_map/all_to_all | solution.py:68
  147.6 3.7 copy-start.3
  158.7 74.8 %all-to-all-start.2 = ((bf16[64,6,2048]{2,1,0:T(8,128)(2,1)}), bf16[64,6,2048]{2,1,0:T(8,128)(2,1)}, u32[]{:S(2)}, u32[]{:S(2)}) async-start(bf16[64,6,2048]{2,1,0:T(8,128)(2,1)} %reshape.116), calls=%async_computation.3 | async-start | bytes 4194304 | tf_op jit(solution)/shard_map/all_to_all | solution.py:83
  183.0 140.4 %reduce-scatter.5.cloned.1.call-start = ((), (), s32[]{:S(2)}) async-start(), calls=%async_computation.7 | async-start | bytes 1769472 | tf_op jit(solution)/shard_map/reduce_scatter | solution.py:87
  242.9 169.7 %reduce-scatter.3.cloned.1.call-start = ((), (), s32[]{:S(2)}) async-start(), calls=%async_computation.6 | async-start | bytes 1769472 | tf_op jit(solution)/shard_map/reduce_scatter | solution.py:77
  246.3 177.1 %copy-start.2 = (s32[128,2]{0,1:T(2,128)S(1)}, s32[128,2]{0,1:T(2,128)}, u32[]{:S(2)}) copy-start(s32[128,2]{0,1:T(2,128)} %param.8) | copy-start | bytes 3076
  325.2 89.1 %all-to-all-start.3 = ((bf16[64,6,256]{2,1,0:T(8,128)(2,1)}), bf16[64,6,256]{2,1,0:T(8,128)(2,1)S(1)}, u32[]{:S(2)}, u32[]{:S(2)}) async-start(bf16[64,6,256]{2,1,0:T(8,128)(2,1)} %reshape.118), calls=%async_computation.5 | async-start | bytes 524288 | tf_op jit(solution)/shard_map/all_to_all | solution.py:88
  414.3 19.6 %all-to-all-start.1 = ((bf16[64,6,256]{2,1,0:T(8,128)(2,1)}), bf16[64,6,256]{2,1,0:T(8,128)(2,1)S(1)}, u32[]{:S(2)}, u32[]{:S(2)}) async-start(bf16[64,6,256]{2,1,0:T(8,128)(2,1)} %reshape.114), calls=%async_computation.2 | async-start | bytes 524288 | tf_op jit(solution)/shard_map/all_to_all | solution.py:78
Sparse Core Ops, SparseCore 0:
  243.0 80.3 reduce-scatter.4
  326.3 86.2 reduce-scatter.2

commit v2 on v1

--- a/solution.py
+++ b/solution.py
@@ -53,8 +53,10 @@
             jnp.bfloat16
         )
 
-    whole_tokens = lax.all_gather(tokens, BLOCK_AXES, axis=1, tiled=True)
-    whole_cot = lax.all_gather(cotangent, BLOCK_AXES, axis=1, tiled=True)
+    stacked = jnp.stack([tokens, cotangent], axis=1)
+    whole_stacked = lax.all_gather(stacked, BLOCK_AXES, axis=2, tiled=True)
+    whole_tokens = whole_stacked[:, 0, :]
+    whole_cot = whole_stacked[:, 1, :]
     whole_grad = (gate_values[:, :, None] * whole_cot[:, None, :].astype(jnp.float32)).astype(
         jnp.bfloat16
     )
@@ -74,13 +76,13 @@
     out_part = jnp.dot(activation, contract_local, preferred_element_type=jnp.float32).astype(
         jnp.bfloat16
     )
+    send_g, out_part = lax.optimization_barrier((send_g, out_part))
     out_rows = lax.psum_scatter(out_part, BLOCK_AXES, scatter_dimension=1, tiled=True)
+    recv_g = lax.all_to_all(send_g, "expert", split_axis=0, concat_axis=0, tiled=True)
     returned_out = lax.all_to_all(
         out_rows.reshape(experts, capacity, width_share), "expert", split_axis=0, concat_axis=0,
         tiled=True,
     )
-
-    recv_g = lax.all_to_all(send_g, "expert", split_axis=0, concat_axis=0, tiled=True)
     grad_activation = transposed_product(recv_g.reshape(slot_count, full_width), contract_local)
     grad_hidden = (grad_activation * derivative).astype(jnp.bfloat16)
     back_part = transposed_product(grad_hidden, expand_local).astype(jnp.bfloat16)

time: 470 us -> 401 us (0.85)
  blocking collectives: 144 us -> 23.9 us
  waiting for transfers between devices: 205 us -> 274 us
  starting transfers between devices: 54.5 us -> 35.2 us
    all_gather x2 -> x0, blocking collectives: 117 us -> none  [the longest x1 67.9 us: per_device(): whole_cot = lax.all_gather(cotangent, BLOCK_AXES, axis=1, tiled=True)]
    reduce_scatter x1, waiting for transfers between devices: 76.2 us -> 0.02 us  [per_device(): lax.psum_scatter(out_part, BLOCK_AXES, scatter_dimension=1, tiled=True)]
    all_to_all x1, waiting for transfers between devices: 42.8 us -> 108 us  [per_device(): lax.all_to_all(send_g, 'expert', split_axis=0, concat_axis=0, tiled=True)]
    all_gather x0 -> x1, waiting for transfers between devices: none -> 58.6 us  [per_device(): whole_stacked = lax.all_gather(stacked, BLOCK_AXES, axis=2, tiled=True)]
    all_to_all x1, waiting for transfers between devices: 0.01 us -> 37.3 us  [per_device(): lax.all_to_all(send_x, 'expert', split_axis=0, concat_axis=0, tiled=True)]
    all_to_all x1, starting transfers between devices: 24.3 us -> 5.56 us  [per_device(): lax.all_to_all(send_g, 'expert', split_axis=0, concat_axis=0, tiled=True)]
    all_to_all x1, waiting for transfers between devices: 9.35 us -> 0.01 us  [per_device(): lax.all_to_all(out_rows.reshape(experts, capacity, width_share), 'expert'...]
    reduce_scatter x1, waiting for transfers between devices: 77.1 us -> 70 us  [per_device(): lax.psum_scatter(back_part, BLOCK_AXES, scatter_dimension=1, tiled=True)]
  transfers between devices with their start and end apart: 6 -> 7, of which waited for: 4 -> 4; matrix products, arithmetic and copies ran while one was open for 6% -> 7% of each run, Pallas kernels for 0% -> 0%
where the time goes in v2:
time: 401 us; the launch traced here: 400 us
  waiting for transfers between devices  274 us (68%)
  starting transfers between devices  35.2 us (9%)
  local copies, waits for them, and re-layouts  30.2 us (8%)
  blocking collectives  23.9 us (6%)
  matrix products  18.4 us (5%)
  between operations  13.9 us (3%)
  other arithmetic  4.44 us (1%)
    all_to_all x1, waiting for transfers between devices, per_device(): lax.all_to_all(send_g, 'expert', split_axis=0, concat_axis=0, tiled=True)  108 us
    reduce_scatter x1, waiting for transfers between devices, per_device(): lax.psum_scatter(back_part, BLOCK_AXES, scatter_dimension=1, tiled=True)  70 us
    all_gather x1, waiting for transfers between devices, per_device(): whole_stacked = lax.all_gather(stacked, BLOCK_AXES, axis=2, tiled=True)  58.6 us
    all_to_all x1, waiting for transfers between devices, per_device(): lax.all_to_all(send_x, 'expert', split_axis=0, concat_axis=0, tiled=True)  37.3 us
    psum x1, blocking collectives, per_device(): gate_grad = lax.psum(partial_dots, BLOCK_AXES)  23.9 us
    all_to_all x1, starting transfers between devices, per_device(): lax.all_to_all(send_x, 'expert', split_axis=0, concat_axis=0, tiled=True)  12.5 us
    all_to_all x1, starting transfers between devices, per_device(): lax.all_to_all(back_rows.reshape(experts, capacity, width_share), 'expert...  11.7 us
  transfers between devices with their start and end apart: 7, of which 4 were waited for; matrix products, arithmetic and copies ran while one was open for 7% of the time, Pallas kernels for 0%

profile of v2, /device:TPU:1, one launch (start us, length us, event | category | flops | bytes accessed | tf_op | source)
XLA Modules:
  0.0 400.2 jit_solution(3012913675446197692)
XLA Ops:
  7.2 0.0 copy-start
  7.2 0.0 all-gather.2.cloned.1.call-start
  7.2 1.7 pad_maximum_fusion
  8.9 0.0 all-gather.2.cloned.1.call-update
  8.9 0.8 copy.16
  9.7 0.1 eq.65
  9.8 0.1 eq.69
  10.0 0.6 reduce-window.6
  10.6 0.2 slice_reduce_fusion
  10.8 0.1 fusion.52
  11.0 58.6 %all-gather.2.cloned.1.call-done = bf16[128,2,2048]{2,0,1:T(8,128)(2,1)} async-done(((bf16[128,2,256]{2,0,1:T(8,128)(2,1)}), bf16[128,2,2048]{2,0,1:T(8,128)(2,1)}) %all-gather.2.cloned.1.call-update) | async-done | bytes 1048592 | tf_op jit(solution)/shard_map/all_gather | solution.py:57
  69.5 1.3 slice_bitcast_fusion
  70.9 1.6 broadcast_in_dim.5
  72.5 2.2 reshape.109
  74.7 3.1 convolution_convert_fusion.2
  77.8 3.7 reshape.110
  81.5 0.0 copy-start.3
  81.5 12.5 %all-to-all-start = ((bf16[64,6,2048]{2,1,0:T(8,128)(2,1)}), bf16[64,6,2048]{2,1,0:T(8,128)(2,1)}, u32[]{:S(2)}, u32[]{:S(2)}) async-start(bf16[64,6,2048]{2,1,0:T(8,128)(2,1)} %reshape.110), calls=%async_computation | async-start | bytes 4194304 | tf_op jit(solution)/shard_map/all_to_all | solution.py:70
  94.0 0.0 copy-done.3
  94.0 0.1 copy.20
  94.1 0.1 mul.112
  94.3 2.5 mul.116
  96.8 3.7 mul.117
  100.5 3.4 convolution_convert_fusion.3
  104.0 3.7 reshape.108
  107.7 37.3 %all-to-all-done = bf16[64,6,2048]{2,1,0:T(8,128)(2,1)} async-done(((bf16[64,6,2048]{2,1,0:T(8,128)(2,1)}), bf16[64,6,2048]{2,1,0:T(8,128)(2,1)}, u32[]{:S(2)}, u32[]{:S(2)}) %all-to-all-start) | async-done | bytes 1572896 | tf_op jit(solution)/shard_map/all_to_all | solution.py:70
  144.9 3.7 reshape.111
  148.6 3.0 fusion.4
  151.7 0.0 copy-done
  151.7 2.2 convolution_convert_fusion.1
  153.9 5.6 %all-to-all-start.2 = ((bf16[64,6,2048]{2,1,0:T(8,128)(2,1)}), bf16[64,6,2048]{2,1,0:T(8,128)(2,1)}, u32[]{:S(2)}, u32[]{:S(2)}) async-start(bf16[64,6,2048]{2,1,0:T(8,128)(2,1)} %reshape.108), calls=%async_computation.3 | async-start | bytes 4194304 | tf_op jit(solution)/shard_map/all_to_all | solution.py:81
  159.5 0.0 reduce-scatter.3.cloned.1.call-start
  159.5 0.7 reduce-scatter.3.cloned.1.call-update
  160.2 0.0 reduce-scatter.5.cloned.1.call-start
  160.3 107.6 %all-to-all-done.2 = bf16[64,6,2048]{2,1,0:T(8,128)(2,1)} async-done(((bf16[64,6,2048]{2,1,0:T(8,128)(2,1)}), bf16[64,6,2048]{2,1,0:T(8,128)(2,1)}, u32[]{:S(2)}, u32[]{:S(2)}) %all-to-all-start.2) | async-done | bytes 1572896 | tf_op jit(solution)/shard_map/all_to_all | solution.py:81
  267.9 3.7 reshape.114
  271.6 5.4 %convolution_convert_fusion = bf16[384,2048]{1,0:T(8,128)(2,1)} fusion(bf16[1,2048,512]{2,1,0:T(8,128)(2,1)} %param.10, bf16[384,2048]{1,0:T(8,128)(2,1)} %reshape.114, bf16[1,512,2048]{2,1,0:T(8,128)(2,1)S(1)} %copy-done, f32[384,512]{1,0:T(8,128)S(1)} %fusion.4), kind=kOutput, calls=%fused_computation | convolution fusion | flops 1615134720 | bytes 8126464 | tf_op jit(solution)/shard_map/dot_general | solution.py:30
  277.0 0.0 copy-start.1
  277.0 0.0 copy-start.2
  277.0 0.0 reduce-scatter.5.cloned.1.call-update
  277.0 0.0 reduce-scatter.3.cloned.1.call-done
  277.0 1.7 reshape.112
  278.7 5.2 %all-to-all-start.1 = ((bf16[64,6,256]{2,1,0:T(8,128)(2,1)}), bf16[64,6,256]{2,1,0:T(8,128)(2,1)S(1)}, u32[]{:S(2)}, u32[]{:S(2)}) async-start(bf16[64,6,256]{2,1,0:T(8,128)(2,1)} %reshape.112), calls=%async_computation.2 | async-start | bytes 524288 | tf_op jit(solution)/shard_map/all_to_all | solution.py:82
  284.0 70.0 %reduce-scatter.5.cloned.1.call-done = bf16[384,256]{1,0:T(8,128)(2,1)} async-done(((bf16[384,2048]{1,0:T(8,128)(2,1)}), bf16[384,256]{1,0:T(8,128)(2,1)}) %reduce-scatter.5.cloned.1.call-update) | async-done | bytes 196624 | tf_op jit(solution)/shard_map/reduce_scatter | solution.py:89
  354.0 1.7 reshape.115
  355.7 0.0 all-to-all-done.1
  355.7 11.7 %all-to-all-start.3 = ((bf16[64,6,256]{2,1,0:T(8,128)(2,1)}), bf16[64,6,256]{2,1,0:T(8,128)(2,1)S(1)}, u32[]{:S(2)}, u32[]{:S(2)}) async-start(bf16[64,6,256]{2,1,0:T(8,128)(2,1)} %reshape.115), calls=%async_computation.5 | async-start | bytes 524288 | tf_op jit(solution)/shard_map/all_to_all | solution.py:90
  367.4 0.0 copy-done.1
  367.4 0.1 reduce_sum.30
  367.6 0.1 copy.19
  367.6 0.0 copy-done.2
  367.7 0.1 reshape.118
  367.7 1.0 multiply_reduce_fusion
  368.8 23.9 %psum.7 = f32[128,2]{0,1:T(2,128)} all-reduce(f32[128,2]{0,1:T(2,128)S(1)} %get-tuple-element.7), channel_id=1, replica_groups=mesh['sec'=2,'section'=4,'expert'=64] {'sec','section'}, use_global_device_ids=true, to_apply=%region_7.8 | all-reduce | flops 256 | bytes 2048 | tf_op jit(solution)/shard_map/psum | solution.py:102
  392.6 0.0 all-to-all-done.3
  392.6 0.1 reshape.119
  392.7 0.3 fusion.40
  393.0 0.6 fusion.49
  (6 shorter events, 0.1 us)
Async XLA Ops:
  7.2 144.5 %copy-start = (bf16[1,512,2048]{2,1,0:T(8,128)(2,1)S(1)}, bf16[1,512,2048]{2,1,0:T(8,128)(2,1)}, u32[]{:S(2)}) copy-start(bf16[1,512,2048]{2,1,0:T(8,128)(2,1)} %param.11) | copy-start | bytes 6291460
  7.2 62.3 %all-gather.2.cloned.1.call-start = ((), (), s32[]{:S(2)}) async-start(), calls=%async_computation.6 | async-start | bytes 1179648 | tf_op jit(solution)/shard_map/all_gather | solution.py:57
  81.5 12.5 %copy-start.3 = (f32[128,2]{0,1:T(2,128)S(1)}, f32[128,2]{0,1:T(2,128)}, u32[]{:S(2)}) copy-start(f32[128,2]{0,1:T(2,128)} %param.9) | copy-start | bytes 3076
  81.5 63.4 %all-to-all-start = ((bf16[64,6,2048]{2,1,0:T(8,128)(2,1)}), bf16[64,6,2048]{2,1,0:T(8,128)(2,1)}, u32[]{:S(2)}, u32[]{:S(2)}) async-start(bf16[64,6,2048]{2,1,0:T(8,128)(2,1)} %reshape.110), calls=%async_computation | async-start | bytes 4194304 | tf_op jit(solution)/shard_map/all_to_all | solution.py:70
  153.9 114.0 %all-to-all-start.2 = ((bf16[64,6,2048]{2,1,0:T(8,128)(2,1)}), bf16[64,6,2048]{2,1,0:T(8,128)(2,1)}, u32[]{:S(2)}, u32[]{:S(2)}) async-start(bf16[64,6,2048]{2,1,0:T(8,128)(2,1)} %reshape.108), calls=%async_computation.3 | async-start | bytes 4194304 | tf_op jit(solution)/shard_map/all_to_all | solution.py:81
  159.5 117.6 %reduce-scatter.3.cloned.1.call-start = ((), (), s32[]{:S(2)}) async-start(), calls=%async_computation.7 | async-start | bytes 1769472 | tf_op jit(solution)/shard_map/reduce_scatter | solution.py:80
  160.2 193.8 %reduce-scatter.5.cloned.1.call-start = ((), (), s32[]{:S(2)}) async-start(), calls=%async_computation.8 | async-start | bytes 1769472 | tf_op jit(solution)/shard_map/reduce_scatter | solution.py:89
  277.0 90.4 %copy-start.1 = (bf16[128,256]{1,0:T(8,128)(2,1)S(1)}, bf16[128,256]{1,0:T(8,128)(2,1)}, u32[]{:S(2)}) copy-start(bf16[128,256]{1,0:T(8,128)(2,1)} %param.7) | copy-start | bytes 196612
  277.0 90.7 %copy-start.2 = (s32[128,2]{0,1:T(2,128)S(1)}, s32[128,2]{0,1:T(2,128)}, u32[]{:S(2)}) copy-start(s32[128,2]{0,1:T(2,128)} %param.8) | copy-start | bytes 3076
  278.7 76.9 %all-to-all-start.1 = ((bf16[64,6,256]{2,1,0:T(8,128)(2,1)}), bf16[64,6,256]{2,1,0:T(8,128)(2,1)S(1)}, u32[]{:S(2)}, u32[]{:S(2)}) async-start(bf16[64,6,256]{2,1,0:T(8,128)(2,1)} %reshape.112), calls=%async_computation.2 | async-start | bytes 524288 | tf_op jit(solution)/shard_map/all_to_all | solution.py:82
  355.7 37.0 %all-to-all-start.3 = ((bf16[64,6,256]{2,1,0:T(8,128)(2,1)}), bf16[64,6,256]{2,1,0:T(8,128)(2,1)S(1)}, u32[]{:S(2)}, u32[]{:S(2)}) async-start(bf16[64,6,256]{2,1,0:T(8,128)(2,1)} %reshape.115), calls=%async_computation.5 | async-start | bytes 524288 | tf_op jit(solution)/shard_map/all_to_all | solution.py:90
Sparse Core Ops, SparseCore 0:
  10.1 59.3 all-gather.1
  163.1 74.6 reduce-scatter.2
  277.1 76.7 reduce-scatter.4

commit v3 on v2

--- a/solution.py
+++ b/solution.py
@@ -67,7 +67,11 @@
     send_g = to_slots(whole_grad.reshape(2 * tok_rows, full_width)).reshape(
         experts, capacity, full_width
     )
-    recv_x = lax.all_to_all(send_x, "expert", split_axis=0, concat_axis=0, tiled=True)
+    recv_xg = lax.all_to_all(
+        jnp.stack([send_x, send_g]), "expert", split_axis=1, concat_axis=1, tiled=True
+    )
+    recv_x = recv_xg[0]
+    recv_g = recv_xg[1]
     hidden = jnp.dot(
         recv_x.reshape(slot_count, full_width), expand_local, preferred_element_type=jnp.float32
     )
@@ -76,9 +80,7 @@
     out_part = jnp.dot(activation, contract_local, preferred_element_type=jnp.float32).astype(
         jnp.bfloat16
     )
-    send_g, out_part = lax.optimization_barrier((send_g, out_part))
     out_rows = lax.psum_scatter(out_part, BLOCK_AXES, scatter_dimension=1, tiled=True)
-    recv_g = lax.all_to_all(send_g, "expert", split_axis=0, concat_axis=0, tiled=True)
     returned_out = lax.all_to_all(
         out_rows.reshape(experts, capacity, width_share), "expert", split_axis=0, concat_axis=0,
         tiled=True,
@@ -87,11 +89,6 @@
     grad_hidden = (grad_activation * derivative).astype(jnp.bfloat16)
     back_part = transposed_product(grad_hidden, expand_local).astype(jnp.bfloat16)
     back_rows = lax.psum_scatter(back_part, BLOCK_AXES, scatter_dimension=1, tiled=True)
-    returned_back = lax.all_to_all(
-        back_rows.reshape(experts, capacity, width_share), "expert", split_axis=0, concat_axis=0,
-        tiled=True,
-    )
-
     out_pairs = jnp.dot(
         placement_matrix,
         returned_out.reshape(slot_count, width_share),
@@ -100,6 +97,11 @@
     combined = jnp.sum(gate_values[:, :, None] * out_pairs, axis=1).astype(jnp.bfloat16)
     partial_dots = jnp.sum(cotangent[:, None, :].astype(jnp.float32) * out_pairs, axis=2)
     gate_grad = lax.psum(partial_dots, BLOCK_AXES)
+    gate_grad, back_rows = lax.optimization_barrier((gate_grad, back_rows))
+    returned_back = lax.all_to_all(
+        back_rows.reshape(experts, capacity, width_share), "expert", split_axis=0, concat_axis=0,
+        tiled=True,
+    )
     back_pairs = jnp.dot(
         placement_matrix,
         returned_back.reshape(slot_count, width_share),

time: 401 us -> 404 us (level)
  blocking collectives: 23.9 us -> 145 us
  waiting for transfers between devices: 274 us -> 157 us
  starting transfers between devices: 35.2 us -> 12.6 us
  local copies, waits for them, and re-layouts: 30.2 us -> 49.3 us
    all_to_all x3 -> x0, waiting for transfers between devices: 145 us -> none  [the longest x1 108 us: per_device(): lax.all_to_all(send_g, 'expert', split_axis=0, concat_axis=0, tiled=True)]
    all_to_all x0 -> x2, blocking collectives: none -> 108 us  [the longest x1 85.5 us: per_device(): lax.all_to_all(jnp.stack([send_x, send_g]), 'expert', split_axis=1, conca...]
    reduce_scatter x1, waiting for transfers between devices: 0.02 us -> 66.1 us  [per_device(): lax.psum_scatter(out_part, BLOCK_AXES, scatter_dimension=1, tiled=True)]
    reduce_scatter x1, waiting for transfers between devices: 70 us -> 21.3 us  [per_device(): lax.psum_scatter(back_part, BLOCK_AXES, scatter_dimension=1, tiled=True)]
    all_to_all x3 -> x0, starting transfers between devices: 29.8 us -> none  [the longest x1 12.5 us: per_device(): lax.all_to_all(send_x, 'expert', split_axis=0, concat_axis=0, tiled=True)]
    another operation x1 -> x6, local copies, waits for them, and re-layouts: 0.01 us -> 18.1 us  [the longest x3 10.7 us: per_device(): jnp.stack([send_x, send_g])]
    slice x1 -> x2, local copies, waits for them, and re-layouts: 0.18 us -> 16.8 us  [the longest x1 16.7 us: per_device(): recv_g = recv_xg[1]]
    reshape x4 -> x0, local copies, waits for them, and re-layouts: 14.8 us -> none  [the longest x1 3.73 us: per_device(): recv_g.reshape(slot_count, full_width)]
  transfers between devices with their start and end apart: 7 -> 4, of which waited for: 4 -> 4; matrix products, arithmetic and copies ran while one was open for 7% -> 4% of each run, Pallas kernels for 0% -> 0%
where the time goes in v3:
time: 404 us; the launch traced here: 403 us
  waiting for transfers between devices  157 us (39%)
  blocking collectives  145 us (36%)
  local copies, waits for them, and re-layouts  49.3 us (12%)
  matrix products  17.3 us (4%)
  between operations  13.9 us (3%)
  starting transfers between devices  12.6 us (3%)
  other arithmetic  7.76 us (2%)
    all_to_all x1, blocking collectives, per_device(): lax.all_to_all(jnp.stack([send_x, send_g]), 'expert', split_axis=1, conca...  85.5 us
    reduce_scatter x1, waiting for transfers between devices, per_device(): lax.psum_scatter(out_part, BLOCK_AXES, scatter_dimension=1, tiled=True)  66.1 us
    all_gather x1, waiting for transfers between devices, per_device(): whole_stacked = lax.all_gather(stacked, BLOCK_AXES, axis=2, tiled=True)  57.6 us
    psum x1, blocking collectives, per_device(): gate_grad = lax.psum(partial_dots, BLOCK_AXES)  37.4 us
    all_to_all x1, blocking collectives, per_device(): lax.all_to_all(back_rows.reshape(experts, capacity, width_share), 'expert...  22.2 us
    reduce_scatter x1, waiting for transfers between devices, per_device(): lax.psum_scatter(back_part, BLOCK_AXES, scatter_dimension=1, tiled=True)  21.3 us
    slice x1, local copies, waits for them, and re-layouts, per_device(): recv_g = recv_xg[1]  16.7 us
    all_to_all x1, starting transfers between devices, per_device(): lax.all_to_all(out_rows.reshape(experts, capacity, width_share), 'expert'...  12.5 us
  transfers between devices with their start and end apart: 4, of which 4 were waited for; matrix products, arithmetic and copies ran while one was open for 4% of the time, Pallas kernels for 0%

profile of v3, /device:TPU:1, one launch (start us, length us, event | category | flops | bytes accessed | tf_op | source)
XLA Modules:
  0.0 403.1 jit_solution(12392211537859151514)
XLA Ops:
  7.2 0.0 copy-start
  7.2 0.0 all-gather.2.cloned.1.call-start
  7.2 1.7 pad_maximum_fusion.1
  8.9 0.0 all-gather.2.cloned.1.call-update
  8.9 0.0 reduce-scatter.3.cloned.1.call-start
  9.0 0.8 copy.24
  9.8 0.1 eq.69
  9.9 0.1 eq.65
  10.1 0.6 reduce-window.6
  10.7 0.2 slice_reduce_fusion.2
  10.9 0.8 copy.28
  11.7 0.1 mul.112
  11.8 0.1 fusion.52
  11.9 57.6 %all-gather.2.cloned.1.call-done = bf16[128,2,2048]{2,0,1:T(8,128)(2,1)} async-done(((bf16[128,2,256]{2,0,1:T(8,128)(2,1)}), bf16[128,2,2048]{2,0,1:T(8,128)(2,1)}) %all-gather.2.cloned.1.call-update) | async-done | bytes 1048592 | tf_op jit(solution)/shard_map/all_gather | solution.py:57
  69.5 1.3 slice_bitcast_fusion.1
  70.9 2.5 mul.116
  73.4 3.7 mul.117
  77.1 3.4 convolution_convert_fusion.2
  80.5 3.7 stack_reshape.7
  84.2 1.6 broadcast_in_dim.5
  85.8 1.5 reshape.96
  87.3 1.9 convolution_convert_fusion.3
  89.2 3.7 stack_reshape.6
  92.8 3.3 pad_maximum_fusion
  96.2 3.3 copy.29
  99.5 85.5 %all_to_all.15 = bf16[2,64,6,2048]{3,0,2,1:T(2,128)(2,1)S(1)} all-to-all(bf16[2,64,6,2048]{3,0,2,1:T(2,128)(2,1)S(1)} %copy.29), channel_id=1, replica_groups=mesh['sec'=2,'section'=4,'expert'=64] {'expert'}, dimensions={1} | all-to-all | bytes 6291456 | tf_op jit(solution)/shard_map/all_to_all | solution.py:70
  185.0 16.7 %slice_reduce_fusion = (bf16[64,6,2048]{2,1,0:T(8,128)(2,1)}, bf16[64,6,2048]{2,1,0:T(8,128)(2,1)}) fusion(bf16[2,64,6,2048]{3,0,2,1:T(2,128)(2,1)S(1)} %all_to_all.15), kind=kLoop, calls=%fused_computation.1 | loop fusion | bytes 6291456 | tf_op jit(solution)/shard_map/slice | solution.py:74
  201.6 3.7 reshape_squeeze.6
  205.4 3.0 fusion.4
  208.4 0.0 copy-done
  208.4 2.2 convolution_convert_fusion.1
  210.6 0.0 reduce-scatter.3.cloned.1.call-update
  210.6 0.0 reduce-scatter.5.cloned.1.call-start
  210.7 3.7 reshape_squeeze.7
  214.4 5.4 %convolution_convert_fusion = bf16[384,2048]{1,0:T(8,128)(2,1)} fusion(bf16[1,2048,512]{2,1,0:T(8,128)(2,1)} %param.10, bf16[384,2048]{1,0:T(8,128)(2,1)} %reshape_squeeze.7, bf16[1,512,2048]{2,1,0:T(8,128)(2,1)S(1)} %copy-done, f32[384,512]{1,0:T(8,128)S(1)} %fusion.4), kind=kOutput, calls=%fused_computation.3 | convolution fusion | flops 1615134720 | bytes 8126464 | tf_op jit(solution)/shard_map/dot_general | solution.py:30
  219.8 0.0 copy-start.1
  219.8 0.0 copy-start.2
  219.9 0.0 copy-start.3
  219.9 0.0 reduce-scatter.5.cloned.1.call-update
  219.9 66.1 %reduce-scatter.3.cloned.1.call-done = bf16[384,256]{1,0:T(8,128)(2,1)} async-done(((bf16[384,2048]{1,0:T(8,128)(2,1)}), bf16[384,256]{1,0:T(8,128)(2,1)}) %reduce-scatter.3.cloned.1.call-update) | async-done | bytes 196624 | tf_op jit(solution)/shard_map/reduce_scatter | solution.py:83
  285.9 1.7 reshape.97
  287.6 12.5 %all-to-all-start.1 = ((bf16[64,6,256]{2,1,0:T(8,128)(2,1)}), bf16[64,6,256]{2,1,0:T(8,128)(2,1)S(1)}, u32[]{:S(2)}, u32[]{:S(2)}) async-start(bf16[64,6,256]{2,1,0:T(8,128)(2,1)} %reshape.97), calls=%async_computation.2 | async-start | bytes 524288 | tf_op jit(solution)/shard_map/all_to_all | solution.py:84
  300.1 0.1 reduce_sum.30
  300.3 0.0 copy-done.1
  300.3 0.1 copy.27
  300.4 0.0 copy-done.2
  300.4 12.2 %all-to-all-done.1 = bf16[64,6,256]{2,1,0:T(8,128)(2,1)S(1)} async-done(((bf16[64,6,256]{2,1,0:T(8,128)(2,1)}), bf16[64,6,256]{2,1,0:T(8,128)(2,1)S(1)}, u32[]{:S(2)}, u32[]{:S(2)}) %all-to-all-start.1) | async-done | bytes 196640 | tf_op jit(solution)/shard_map/all_to_all | solution.py:84
  312.5 0.1 reshape.102
  312.6 0.0 copy-done.3
  312.6 1.0 multiply_reduce_fusion
  313.6 37.4 %psum.7 = f32[128,2]{0,1:T(2,128)} all-reduce(f32[128,2]{0,1:T(2,128)S(1)} %get-tuple-element.9), channel_id=1, replica_groups=mesh['sec'=2,'section'=4,'expert'=64] {'sec','section'}, use_global_device_ids=true, to_apply=%region_6.7 | all-reduce | flops 256 | bytes 2048 | tf_op jit(solution)/shard_map/psum | solution.py:99
  351.0 21.3 %reduce-scatter.5.cloned.1.call-done = bf16[384,256]{1,0:T(8,128)(2,1)} async-done(((bf16[384,2048]{1,0:T(8,128)(2,1)}), bf16[384,256]{1,0:T(8,128)(2,1)}) %reduce-scatter.5.cloned.1.call-update) | async-done | bytes 196624 | tf_op jit(solution)/shard_map/reduce_scatter | solution.py:91
  372.3 1.0 reshape.99
  373.3 22.2 %all_to_all.16 = bf16[64,6,256]{2,1,0:T(8,128)(2,1)S(1)} all-to-all(bf16[64,6,256]{2,1,0:T(8,128)(2,1)S(1)} %reshape.99), channel_id=1, replica_groups=mesh['sec'=2,'section'=4,'expert'=64] {'expert'}, dimensions={0} | all-to-all | bytes 393216 | tf_op jit(solution)/shard_map/all_to_all | solution.py:101
  395.5 0.1 reshape.103
  395.6 0.3 fusion.40
  395.9 0.6 fusion.49
  (6 shorter events, 0.1 us)
Async XLA Ops:
  7.2 201.2 %copy-start = (bf16[1,512,2048]{2,1,0:T(8,128)(2,1)S(1)}, bf16[1,512,2048]{2,1,0:T(8,128)(2,1)}, u32[]{:S(2)}) copy-start(bf16[1,512,2048]{2,1,0:T(8,128)(2,1)} %param.11) | copy-start | bytes 6291460
  7.2 62.3 %all-gather.2.cloned.1.call-start = ((), (), s32[]{:S(2)}) async-start(), calls=%async_computation.5 | async-start | bytes 1179648 | tf_op jit(solution)/shard_map/all_gather | solution.py:57
  8.9 277.0 %reduce-scatter.3.cloned.1.call-start = ((), (), s32[]{:S(2)}) async-start(), calls=%async_computation.6 | async-start | bytes 1769472 | tf_op jit(solution)/shard_map/reduce_scatter | solution.py:83
  210.6 161.7 %reduce-scatter.5.cloned.1.call-start = ((), (), s32[]{:S(2)}) async-start(), calls=%async_computation.7 | async-start | bytes 1769472 | tf_op jit(solution)/shard_map/reduce_scatter | solution.py:91
  219.8 80.4 %copy-start.1 = (bf16[128,256]{1,0:T(8,128)(2,1)S(1)}, bf16[128,256]{1,0:T(8,128)(2,1)}, u32[]{:S(2)}) copy-start(bf16[128,256]{1,0:T(8,128)(2,1)} %param.7) | copy-start | bytes 196612
  219.8 80.5 %copy-start.2 = (s32[128,2]{0,1:T(2,128)S(1)}, s32[128,2]{0,1:T(2,128)}, u32[]{:S(2)}) copy-start(s32[128,2]{0,1:T(2,128)} %param.8) | copy-start | bytes 3076
  219.9 92.8 %copy-start.3 = (f32[128,2]{0,1:T(2,128)S(1)}, f32[128,2]{0,1:T(2,128)}, u32[]{:S(2)}) copy-start(f32[128,2]{0,1:T(2,128)} %param.9) | copy-start | bytes 3076
  287.6 24.9 %all-to-all-start.1 = ((bf16[64,6,256]{2,1,0:T(8,128)(2,1)}), bf16[64,6,256]{2,1,0:T(8,128)(2,1)S(1)}, u32[]{:S(2)}, u32[]{:S(2)}) async-start(bf16[64,6,256]{2,1,0:T(8,128)(2,1)} %reshape.97), calls=%async_computation.2 | async-start | bytes 524288 | tf_op jit(solution)/shard_map/all_to_all | solution.py:84
Sparse Core Ops, SparseCore 0:
  10.1 59.3 all-gather.1
  210.8 75.1 reduce-scatter.2
  288.8 83.4 reduce-scatter.4

commit v4 on v3

--- a/solution.py
+++ b/solution.py
@@ -67,11 +67,15 @@
     send_g = to_slots(whole_grad.reshape(2 * tok_rows, full_width)).reshape(
         experts, capacity, full_width
     )
-    recv_xg = lax.all_to_all(
-        jnp.stack([send_x, send_g]), "expert", split_axis=1, concat_axis=1, tiled=True
+    lane = 128
+    chunk_rows = capacity * full_width // lane
+    send_xg = jnp.concatenate(
+        [send_x.reshape(experts, chunk_rows, lane), send_g.reshape(experts, chunk_rows, lane)],
+        axis=1,
     )
-    recv_x = recv_xg[0]
-    recv_g = recv_xg[1]
+    recv_xg = lax.all_to_all(send_xg, "expert", split_axis=0, concat_axis=0, tiled=True)
+    recv_x = recv_xg[:, :chunk_rows].reshape(slot_count, full_width)
+    recv_g = recv_xg[:, chunk_rows:].reshape(slot_count, full_width)
     hidden = jnp.dot(
         recv_x.reshape(slot_count, full_width), expand_local, preferred_element_type=jnp.float32
     )

time: 404 us -> 387 us (0.958)
  local copies, waits for them, and re-layouts: 49.3 us -> 31.3 us
  waiting for transfers between devices: 157 us -> 164 us
  blocking collectives: 145 us -> 139 us
    slice x2, local copies, waits for them, and re-layouts: 16.8 us -> 2.05 us  [the longest x1 1.87 us: per_device(): recv_g = recv_xg[:, chunk_rows:].reshape(slot_count, full_width)]
    another operation x6 -> x3, local copies, waits for them, and re-layouts: 18.1 us -> 7.53 us  [the longest x1 3.77 us: per_device(): send_g.reshape(experts, chunk_rows, lane)]
    reduce_scatter x1, waiting for transfers between devices: 21.3 us -> 30.2 us  [per_device(): lax.psum_scatter(back_part, BLOCK_AXES, scatter_dimension=1, tiled=True)]
    reshape x0 -> x2, local copies, waits for them, and re-layouts: none -> 7.37 us  [the longest x1 3.69 us: per_device(): recv_g = recv_xg[:, chunk_rows:].reshape(slot_count, full_width)]
where the time goes in v4:
time: 387 us; the launch traced here: 385 us
  waiting for transfers between devices  164 us (42%)
  blocking collectives  139 us (36%)
  local copies, waits for them, and re-layouts  31.3 us (8%)
  matrix products  17.2 us (4%)
  between operations  13.9 us (4%)
  starting transfers between devices  12.6 us (3%)
  other arithmetic  6.6 us (2%)
    all_to_all x1, blocking collectives, per_device(): lax.all_to_all(send_xg, 'expert', split_axis=0, concat_axis=0, tiled=True)  85.5 us
    reduce_scatter x1, waiting for transfers between devices, per_device(): lax.psum_scatter(out_part, BLOCK_AXES, scatter_dimension=1, tiled=True)  65.3 us
    all_gather x1, waiting for transfers between devices, per_device(): whole_stacked = lax.all_gather(stacked, BLOCK_AXES, axis=2, tiled=True)  57.6 us
    psum x1, blocking collectives, per_device(): gate_grad = lax.psum(partial_dots, BLOCK_AXES)  33.7 us
    reduce_scatter x1, waiting for transfers between devices, per_device(): lax.psum_scatter(back_part, BLOCK_AXES, scatter_dimension=1, tiled=True)  30.2 us
    all_to_all x1, blocking collectives, per_device(): lax.all_to_all(back_rows.reshape(experts, capacity, width_share), 'expert...  20.3 us
    all_to_all x1, starting transfers between devices, per_device(): lax.all_to_all(out_rows.reshape(experts, capacity, width_share), 'expert'...  12.5 us
    all_to_all x1, waiting for transfers between devices, per_device(): lax.all_to_all(out_rows.reshape(experts, capacity, width_share), 'expert'...  11 us
  transfers between devices with their start and end apart: 4, of which 4 were waited for; matrix products, arithmetic and copies ran while one was open for 4% of the time, Pallas kernels for 0%

profile of v4, /device:TPU:1, one launch (start us, length us, event | category | flops | bytes accessed | tf_op | source)
XLA Modules:
  0.0 385.1 jit_solution(17963025313209641403)
XLA Ops:
  7.2 0.0 copy-start
  7.2 0.0 all-gather.2.cloned.1.call-start
  7.2 1.7 pad_maximum_fusion.1
  8.9 0.0 all-gather.2.cloned.1.call-update
  8.9 0.0 reduce-scatter.3.cloned.1.call-start
  9.0 0.8 copy.16
  9.8 0.1 eq.69
  9.9 0.1 eq.65
  10.1 0.6 reduce-window.6
  10.7 0.2 slice_reduce_fusion
  10.9 0.8 copy.20
  11.7 0.1 mul.112
  11.8 0.1 fusion.52
  11.9 57.6 %all-gather.2.cloned.1.call-done = bf16[128,2,2048]{2,0,1:T(8,128)(2,1)} async-done(((bf16[128,2,256]{2,0,1:T(8,128)(2,1)}), bf16[128,2,2048]{2,0,1:T(8,128)(2,1)}) %all-gather.2.cloned.1.call-update) | async-done | bytes 1048592 | tf_op jit(solution)/shard_map/all_gather | solution.py:57
  69.5 1.3 slice_bitcast_fusion.1
  70.9 2.5 mul.116
  73.4 3.7 mul.117
  77.1 3.4 convolution_convert_fusion.2
  80.5 3.8 reshape_reshape.7
  84.3 1.6 broadcast_in_dim.5
  85.9 1.5 reshape.102
  87.3 1.8 convolution_convert_fusion.3
  89.2 3.8 reshape_reshape.6
  92.9 2.2 pad_maximum_fusion
  95.1 85.5 %all_to_all.15 = bf16[64,192,128]{2,1,0:T(8,128)(2,1)S(1)} all-to-all(bf16[64,192,128]{2,1,0:T(8,128)(2,1)S(1)} %pad_maximum_fusion), channel_id=1, replica_groups=mesh['sec'=2,'section'=4,'expert'=64] {'expert'}, dimensions={0} | all-to-all | bytes 6291456 | tf_op jit(solution)/shard_map/all_to_all | solution.py:76
  180.6 1.9 fusion.63
  182.5 3.7 reshape.103
  186.2 3.0 fusion.4
  189.2 0.0 copy-done
  189.2 2.2 convolution_convert_fusion.1
  191.4 0.0 reduce-scatter.3.cloned.1.call-update
  191.5 0.0 reduce-scatter.5.cloned.1.call-start
  191.5 3.7 reshape.106
  195.2 5.4 %convolution_convert_fusion = bf16[384,2048]{1,0:T(8,128)(2,1)} fusion(bf16[1,2048,512]{2,1,0:T(8,128)(2,1)} %param.10, bf16[384,2048]{1,0:T(8,128)(2,1)} %reshape.106, bf16[1,512,2048]{2,1,0:T(8,128)(2,1)S(1)} %copy-done, f32[384,512]{1,0:T(8,128)S(1)} %fusion.4), kind=kOutput, calls=%fused_computation.1 | convolution fusion | flops 1615134720 | bytes 8126464 | tf_op jit(solution)/shard_map/dot_general | solution.py:30
  200.6 0.0 copy-start.1
  200.6 0.0 copy-start.2
  200.6 0.0 copy-start.3
  200.6 0.0 reduce-scatter.5.cloned.1.call-update
  200.6 65.3 %reduce-scatter.3.cloned.1.call-done = bf16[384,256]{1,0:T(8,128)(2,1)} async-done(((bf16[384,2048]{1,0:T(8,128)(2,1)}), bf16[384,256]{1,0:T(8,128)(2,1)}) %reduce-scatter.3.cloned.1.call-update) | async-done | bytes 196624 | tf_op jit(solution)/shard_map/reduce_scatter | solution.py:87
  266.0 1.7 reshape.104
  267.7 12.5 %all-to-all-start.1 = ((bf16[64,6,256]{2,1,0:T(8,128)(2,1)}), bf16[64,6,256]{2,1,0:T(8,128)(2,1)S(1)}, u32[]{:S(2)}, u32[]{:S(2)}) async-start(bf16[64,6,256]{2,1,0:T(8,128)(2,1)} %reshape.104), calls=%async_computation.2 | async-start | bytes 524288 | tf_op jit(solution)/shard_map/all_to_all | solution.py:88
  280.1 0.1 reduce_sum.30
  280.3 0.0 copy-done.1
  280.3 0.1 copy.19
  280.4 0.0 copy-done.2
  280.4 11.0 %all-to-all-done.1 = bf16[64,6,256]{2,1,0:T(8,128)(2,1)S(1)} async-done(((bf16[64,6,256]{2,1,0:T(8,128)(2,1)}), bf16[64,6,256]{2,1,0:T(8,128)(2,1)S(1)}, u32[]{:S(2)}, u32[]{:S(2)}) %all-to-all-start.1) | async-done | bytes 196640 | tf_op jit(solution)/shard_map/all_to_all | solution.py:88
  291.4 0.1 reshape.110
  291.4 0.0 copy-done.3
  291.4 1.0 multiply_reduce_fusion
  292.4 33.7 %psum.7 = f32[128,2]{0,1:T(2,128)} all-reduce(f32[128,2]{0,1:T(2,128)S(1)} %get-tuple-element.7), channel_id=1, replica_groups=mesh['sec'=2,'section'=4,'expert'=64] {'sec','section'}, use_global_device_ids=true, to_apply=%region_6.7 | all-reduce | flops 256 | bytes 2048 | tf_op jit(solution)/shard_map/psum | solution.py:103
  326.1 30.2 %reduce-scatter.5.cloned.1.call-done = bf16[384,256]{1,0:T(8,128)(2,1)} async-done(((bf16[384,2048]{1,0:T(8,128)(2,1)}), bf16[384,256]{1,0:T(8,128)(2,1)}) %reduce-scatter.5.cloned.1.call-update) | async-done | bytes 196624 | tf_op jit(solution)/shard_map/reduce_scatter | solution.py:95
  356.3 1.0 reshape.107
  357.3 20.3 %all_to_all.16 = bf16[64,6,256]{2,1,0:T(8,128)(2,1)S(1)} all-to-all(bf16[64,6,256]{2,1,0:T(8,128)(2,1)S(1)} %reshape.107), channel_id=1, replica_groups=mesh['sec'=2,'section'=4,'expert'=64] {'expert'}, dimensions={0} | all-to-all | bytes 393216 | tf_op jit(solution)/shard_map/all_to_all | solution.py:105
  377.6 0.1 reshape.111
  377.6 0.3 fusion.40
  377.9 0.6 fusion.49
  (6 shorter events, 0.1 us)
Async XLA Ops:
  7.2 182.1 %copy-start = (bf16[1,512,2048]{2,1,0:T(8,128)(2,1)S(1)}, bf16[1,512,2048]{2,1,0:T(8,128)(2,1)}, u32[]{:S(2)}) copy-start(bf16[1,512,2048]{2,1,0:T(8,128)(2,1)} %param.11) | copy-start | bytes 6291460
  7.2 62.3 %all-gather.2.cloned.1.call-start = ((), (), s32[]{:S(2)}) async-start(), calls=%async_computation.5 | async-start | bytes 1179648 | tf_op jit(solution)/shard_map/all_gather | solution.py:57
  8.9 257.1 %reduce-scatter.3.cloned.1.call-start = ((), (), s32[]{:S(2)}) async-start(), calls=%async_computation.6 | async-start | bytes 1769472 | tf_op jit(solution)/shard_map/reduce_scatter | solution.py:87
  191.5 164.9 %reduce-scatter.5.cloned.1.call-start = ((), (), s32[]{:S(2)}) async-start(), calls=%async_computation.7 | async-start | bytes 1769472 | tf_op jit(solution)/shard_map/reduce_scatter | solution.py:95
  200.6 79.7 %copy-start.1 = (bf16[128,256]{1,0:T(8,128)(2,1)S(1)}, bf16[128,256]{1,0:T(8,128)(2,1)}, u32[]{:S(2)}) copy-start(bf16[128,256]{1,0:T(8,128)(2,1)} %param.7) | copy-start | bytes 196612
  200.6 79.8 %copy-start.2 = (s32[128,2]{0,1:T(2,128)S(1)}, s32[128,2]{0,1:T(2,128)}, u32[]{:S(2)}) copy-start(s32[128,2]{0,1:T(2,128)} %param.8) | copy-start | bytes 3076
  200.6 90.8 %copy-start.3 = (f32[128,2]{0,1:T(2,128)S(1)}, f32[128,2]{0,1:T(2,128)}, u32[]{:S(2)}) copy-start(f32[128,2]{0,1:T(2,128)} %param.9) | copy-start | bytes 3076
  267.7 23.7 %all-to-all-start.1 = ((bf16[64,6,256]{2,1,0:T(8,128)(2,1)}), bf16[64,6,256]{2,1,0:T(8,128)(2,1)S(1)}, u32[]{:S(2)}, u32[]{:S(2)}) async-start(bf16[64,6,256]{2,1,0:T(8,128)(2,1)} %reshape.104), calls=%async_computation.2 | async-start | bytes 524288 | tf_op jit(solution)/shard_map/all_to_all | solution.py:88
Sparse Core Ops, SparseCore 0:
  10.1 59.3 all-gather.1
  191.6 74.3 reduce-scatter.2
  268.8 87.4 reduce-scatter.4

commit v5 on v4

--- a/solution.py
+++ b/solution.py
@@ -84,15 +84,21 @@
     out_part = jnp.dot(activation, contract_local, preferred_element_type=jnp.float32).astype(
         jnp.bfloat16
     )
+    grad_activation = transposed_product(recv_g.reshape(slot_count, full_width), contract_local)
+    grad_hidden = (grad_activation * derivative).astype(jnp.bfloat16)
+    back_part = transposed_product(grad_hidden, expand_local).astype(jnp.bfloat16)
+    out_part, back_part = lax.optimization_barrier((out_part, back_part))
     out_rows = lax.psum_scatter(out_part, BLOCK_AXES, scatter_dimension=1, tiled=True)
+    block_count = full_width // width_share
+    back_blocks = lax.all_to_all(
+        back_part.reshape(slot_count, block_count, width_share), BLOCK_AXES, 1, 1, tiled=True
+    )
+    out_rows, back_blocks = lax.optimization_barrier((out_rows, back_blocks))
+    back_rows = jnp.sum(back_blocks.astype(jnp.float32), axis=1).astype(jnp.bfloat16)
     returned_out = lax.all_to_all(
         out_rows.reshape(experts, capacity, width_share), "expert", split_axis=0, concat_axis=0,
         tiled=True,
     )
-    grad_activation = transposed_product(recv_g.reshape(slot_count, full_width), contract_local)
-    grad_hidden = (grad_activation * derivative).astype(jnp.bfloat16)
-    back_part = transposed_product(grad_hidden, expand_local).astype(jnp.bfloat16)
-    back_rows = lax.psum_scatter(back_part, BLOCK_AXES, scatter_dimension=1, tiled=True)
     out_pairs = jnp.dot(
         placement_matrix,
         returned_out.reshape(slot_count, width_share),
@@ -101,7 +107,6 @@
     combined = jnp.sum(gate_values[:, :, None] * out_pairs, axis=1).astype(jnp.bfloat16)
     partial_dots = jnp.sum(cotangent[:, None, :].astype(jnp.float32) * out_pairs, axis=2)
     gate_grad = lax.psum(partial_dots, BLOCK_AXES)
-    gate_grad, back_rows = lax.optimization_barrier((gate_grad, back_rows))
     returned_back = lax.all_to_all(
         back_rows.reshape(experts, capacity, width_share), "expert", split_axis=0, concat_axis=0,
         tiled=True,

time: 387 us -> 424 us (1.096)
  waiting for transfers between devices: 164 us -> 218 us
  blocking collectives: 139 us -> 112 us
  starting transfers between devices: 12.6 us -> 20.3 us
    reduce_scatter x1, waiting for transfers between devices: 65.3 us -> 140 us  [per_device(): lax.psum_scatter(out_part, BLOCK_AXES, scatter_dimension=1, tiled=True)]
    reduce_scatter x1 -> x0, waiting for transfers between devices: 30.2 us -> none  [per_device(): lax.psum_scatter(back_part, BLOCK_AXES, scatter_dimension=1, tiled=True)]
    all_to_all x1 -> x0, blocking collectives: 20.3 us -> none  [per_device(): lax.all_to_all(back_rows.reshape(experts, capacity, width_share), 'expert...]
    all_to_all x0 -> x2, starting transfers between devices: none -> 14.6 us  [the longest x1 8.5 us: per_device(): lax.all_to_all(back_rows.reshape(experts, capacity, width_share), 'expert...]
    all_to_all x0 -> x2, waiting for transfers between devices: none -> 10.9 us  [the longest x1 10.9 us: per_device(): lax.all_to_all(back_rows.reshape(experts, capacity, width_share), 'expert...]
    psum x1, blocking collectives: 33.7 us -> 26.1 us  [per_device(): gate_grad = lax.psum(partial_dots, BLOCK_AXES)]
    all_to_all x1, starting transfers between devices: 12.5 us -> 5.58 us  [per_device(): lax.all_to_all(out_rows.reshape(experts, capacity, width_share), 'expert'...]
  transfers between devices with their start and end apart: 4 -> 5, of which waited for: 4 -> 4; matrix products, arithmetic and copies ran while one was open for 4% -> 1% of each run, Pallas kernels for 0% -> 0%
where the time goes in v5:
time: 424 us; the launch traced here: 423 us
  waiting for transfers between devices  218 us (51%)
  blocking collectives  112 us (26%)
  local copies, waits for them, and re-layouts  32.8 us (8%)
  starting transfers between devices  20.3 us (5%)
  matrix products  17.2 us (4%)
  between operations  14.2 us (3%)
  other arithmetic  8.3 us (2%)
    reduce_scatter x1, waiting for transfers between devices, per_device(): lax.psum_scatter(out_part, BLOCK_AXES, scatter_dimension=1, tiled=True)  140 us
    all_to_all x1, blocking collectives, per_device(): lax.all_to_all(send_xg, 'expert', split_axis=0, concat_axis=0, tiled=True)  85.5 us
    all_gather x1, waiting for transfers between devices, per_device(): whole_stacked = lax.all_gather(stacked, BLOCK_AXES, axis=2, tiled=True)  57.6 us
    psum x1, blocking collectives, per_device(): gate_grad = lax.psum(partial_dots, BLOCK_AXES)  26.1 us
    all_to_all x1, waiting for transfers between devices, per_device(): lax.all_to_all(back_rows.reshape(experts, capacity, width_share), 'expert...  10.9 us
    all_to_all x1, waiting for transfers between devices, per_device(): lax.all_to_all(out_rows.reshape(experts, capacity, width_share), 'expert'...  9.3 us
    all_to_all x1, starting transfers between devices, per_device(): lax.all_to_all(back_rows.reshape(experts, capacity, width_share), 'expert...  8.5 us
  transfers between devices with their start and end apart: 5, of which 4 were waited for; matrix products, arithmetic and copies ran while one was open for 1% of the time, Pallas kernels for 0%

profile of v5, /device:TPU:1, one launch (start us, length us, event | category | flops | bytes accessed | tf_op | source)
XLA Modules:
  0.0 422.7 jit_solution(2464353978097156470)
XLA Ops:
  7.2 0.0 copy-start
  7.2 0.0 all-gather.2.cloned.1.call-start
  7.2 1.7 pad_maximum_fusion.1
  8.9 0.0 all-gather.2.cloned.1.call-update
  8.9 0.8 copy.24
  9.7 0.1 eq.69
  9.8 0.1 eq.65
  10.0 0.6 reduce-window.6
  10.6 0.2 slice_reduce_fusion
  10.8 0.8 copy.28
  11.6 0.1 mul.112
  11.8 0.1 fusion.52
  11.9 57.6 %all-gather.2.cloned.1.call-done = bf16[128,2,2048]{2,0,1:T(8,128)(2,1)} async-done(((bf16[128,2,256]{2,0,1:T(8,128)(2,1)}), bf16[128,2,2048]{2,0,1:T(8,128)(2,1)}) %all-gather.2.cloned.1.call-update) | async-done | bytes 1048592 | tf_op jit(solution)/shard_map/all_gather | solution.py:57
  69.5 1.3 slice_bitcast_fusion.1
  70.9 2.5 mul.116
  73.4 3.7 mul.117
  77.1 3.4 convolution_convert_fusion.2
  80.5 3.8 reshape_reshape.7
  84.3 1.6 broadcast_in_dim.5
  85.9 1.5 reshape.105
  87.3 1.8 convolution_convert_fusion.3
  89.2 3.8 reshape_reshape.6
  92.9 2.2 pad_maximum_fusion
  95.1 85.5 %all_to_all.20 = bf16[64,192,128]{2,1,0:T(8,128)(2,1)S(1)} all-to-all(bf16[64,192,128]{2,1,0:T(8,128)(2,1)S(1)} %pad_maximum_fusion), channel_id=1, replica_groups=mesh['sec'=2,'section'=4,'expert'=64] {'expert'}, dimensions={0} | all-to-all | bytes 6291456 | tf_op jit(solution)/shard_map/all_to_all | solution.py:76
  180.6 1.9 fusion.63
  182.5 3.7 reshape.106
  186.2 3.7 reshape.107
  189.9 3.0 fusion.4
  192.9 0.0 copy-done
  192.9 2.2 convolution_convert_fusion.1
  195.2 5.4 %convolution_convert_fusion = bf16[384,2048]{1,0:T(8,128)(2,1)} fusion(bf16[1,2048,512]{2,1,0:T(8,128)(2,1)} %param.10, bf16[384,2048]{1,0:T(8,128)(2,1)} %reshape.107, bf16[1,512,2048]{2,1,0:T(8,128)(2,1)S(1)} %copy-done, f32[384,512]{1,0:T(8,128)S(1)} %fusion.4), kind=kOutput, calls=%fused_computation.1 | convolution fusion | flops 1615134720 | bytes 8126464 | tf_op jit(solution)/shard_map/dot_general | solution.py:30
  200.5 2.7 copy.34
  203.2 6.1 %all-to-all-start.1 = ((bf16[384,8,256]{2,0,1:T(8,128)(2,1)}), bf16[384,8,256]{2,0,1:T(8,128)(2,1)}, u32[]{:S(2)}, u32[]{:S(2)}) async-start(bf16[384,8,256]{2,0,1:T(8,128)(2,1)} %bitcast.61), calls=%async_computation.2 | async-start | bytes 3145728 | tf_op jit(solution)/shard_map/all_to_all | solution.py:93
  209.3 0.0 reduce-scatter.2.cloned.1.call-start
  209.3 0.7 reduce-scatter.2.cloned.1.call-update
  210.1 0.0 copy-start.1
  210.1 0.0 copy-start.3
  210.1 139.7 %reduce-scatter.2.cloned.1.call-done = bf16[384,256]{1,0:T(8,128)(2,1)} async-done(((bf16[384,2048]{1,0:T(8,128)(2,1)}), bf16[384,256]{1,0:T(8,128)(2,1)}) %reduce-scatter.2.cloned.1.call-update) | async-done | bytes 196624 | tf_op jit(solution)/shard_map/reduce_scatter | solution.py:91
  349.8 0.0 copy-start.2
  349.8 0.0 all-to-all-done.1
  349.8 1.7 reduce_sum.44
  351.5 0.0 copy-start.4
  351.5 0.8 reshape.111
  352.3 8.5 %all-to-all-start.3 = ((bf16[64,6,256]{2,1,0:T(8,128)(2,1)}), bf16[64,6,256]{2,1,0:T(8,128)(2,1)S(1)}, u32[]{:S(2)}, u32[]{:S(2)}) async-start(bf16[64,6,256]{2,1,0:T(8,128)(2,1)} %reshape.111), calls=%async_computation.4 | async-start | bytes 524288 | tf_op jit(solution)/shard_map/all_to_all | solution.py:110
  360.8 0.0 copy-done.2
  360.8 0.8 reshape.109
  361.6 10.9 %all-to-all-done.3 = bf16[64,6,256]{2,1,0:T(8,128)(2,1)S(1)} async-done(((bf16[64,6,256]{2,1,0:T(8,128)(2,1)}), bf16[64,6,256]{2,1,0:T(8,128)(2,1)S(1)}, u32[]{:S(2)}, u32[]{:S(2)}) %all-to-all-start.3) | async-done | bytes 196640 | tf_op jit(solution)/shard_map/all_to_all | solution.py:110
  372.5 5.6 %all-to-all-start.2 = ((bf16[64,6,256]{2,1,0:T(8,128)(2,1)}), bf16[64,6,256]{2,1,0:T(8,128)(2,1)S(1)}, u32[]{:S(2)}, u32[]{:S(2)}) async-start(bf16[64,6,256]{2,1,0:T(8,128)(2,1)} %reshape.109), calls=%async_computation.3 | async-start | bytes 524288 | tf_op jit(solution)/shard_map/all_to_all | solution.py:98
  378.1 0.1 reduce_sum.42
  378.2 0.0 copy-done.1
  378.2 0.1 copy.27
  378.3 0.0 copy-done.3
  378.3 0.1 reshape.115
  378.4 0.3 fusion.40
  378.7 0.6 fusion.49
  379.3 9.3 %all-to-all-done.2 = bf16[64,6,256]{2,1,0:T(8,128)(2,1)S(1)} async-done(((bf16[64,6,256]{2,1,0:T(8,128)(2,1)}), bf16[64,6,256]{2,1,0:T(8,128)(2,1)S(1)}, u32[]{:S(2)}, u32[]{:S(2)}) %all-to-all-start.2) | async-done | bytes 196640 | tf_op jit(solution)/shard_map/all_to_all | solution.py:98
  388.6 0.1 reshape.114
  388.7 0.0 copy-done.4
  388.7 1.0 multiply_reduce_fusion
  389.7 26.1 %psum.7 = f32[128,2]{0,1:T(2,128)} all-reduce(f32[128,2]{0,1:T(2,128)S(1)} %get-tuple-element.11), channel_id=1, replica_groups=mesh['sec'=2,'section'=4,'expert'=64] {'sec','section'}, use_global_device_ids=true, to_apply=%region_7.8 | all-reduce | flops 256 | bytes 2048 | tf_op jit(solution)/shard_map/psum | solution.py:109
  (6 shorter events, 0.1 us)
Async XLA Ops:
  7.2 185.8 %copy-start = (bf16[1,512,2048]{2,1,0:T(8,128)(2,1)S(1)}, bf16[1,512,2048]{2,1,0:T(8,128)(2,1)}, u32[]{:S(2)}) copy-start(bf16[1,512,2048]{2,1,0:T(8,128)(2,1)} %param.11) | copy-start | bytes 6291460
  7.2 62.3 %all-gather.2.cloned.1.call-start = ((), (), s32[]{:S(2)}) async-start(), calls=%async_computation.5 | async-start | bytes 1179648 | tf_op jit(solution)/shard_map/all_gather | solution.py:57
  203.2 146.6 %all-to-all-start.1 = ((bf16[384,8,256]{2,0,1:T(8,128)(2,1)}), bf16[384,8,256]{2,0,1:T(8,128)(2,1)}, u32[]{:S(2)}, u32[]{:S(2)}) async-start(bf16[384,8,256]{2,0,1:T(8,128)(2,1)} %bitcast.61), calls=%async_computation.2 | async-start | bytes 3145728 | tf_op jit(solution)/shard_map/all_to_all | solution.py:93
  209.3 140.5 %reduce-scatter.2.cloned.1.call-start = ((), (), s32[]{:S(2)}) async-start(), calls=%async_computation.6 | async-start | bytes 1769472 | tf_op jit(solution)/shard_map/reduce_scatter | solution.py:91
  210.1 168.1 %copy-start.1 = (bf16[128,256]{1,0:T(8,128)(2,1)S(1)}, bf16[128,256]{1,0:T(8,128)(2,1)}, u32[]{:S(2)}) copy-start(bf16[128,256]{1,0:T(8,128)(2,1)} %param.7) | copy-start | bytes 196612
  210.1 168.2 %copy-start.3 = (s32[128,2]{0,1:T(2,128)S(1)}, s32[128,2]{0,1:T(2,128)}, u32[]{:S(2)}) copy-start(s32[128,2]{0,1:T(2,128)} %param.8) | copy-start | bytes 3076
  349.8 11.0 %copy-start.2 = (bf16[384,256]{1,0:T(8,128)(2,1)S(1)}, bf16[384,256]{1,0:T(8,128)(2,1)}, u32[]{:S(2)}) copy-start(bf16[384,256]{1,0:T(8,128)(2,1)} %reduce-scatter.2.cloned.1.call-done) | copy-start | bytes 589828
  351.5 37.2 %copy-start.4 = (f32[128,2]{0,1:T(2,128)S(1)}, f32[128,2]{0,1:T(2,128)}, u32[]{:S(2)}) copy-start(f32[128,2]{0,1:T(2,128)} %param.9) | copy-start | bytes 3076
  352.3 20.2 %all-to-all-start.3 = ((bf16[64,6,256]{2,1,0:T(8,128)(2,1)}), bf16[64,6,256]{2,1,0:T(8,128)(2,1)S(1)}, u32[]{:S(2)}, u32[]{:S(2)}) async-start(bf16[64,6,256]{2,1,0:T(8,128)(2,1)} %reshape.111), calls=%async_computation.4 | async-start | bytes 524288 | tf_op jit(solution)/shard_map/all_to_all | solution.py:110
  372.5 16.2 %all-to-all-start.2 = ((bf16[64,6,256]{2,1,0:T(8,128)(2,1)}), bf16[64,6,256]{2,1,0:T(8,128)(2,1)S(1)}, u32[]{:S(2)}, u32[]{:S(2)}) async-start(bf16[64,6,256]{2,1,0:T(8,128)(2,1)} %reshape.109), calls=%async_computation.3 | async-start | bytes 524288 | tf_op jit(solution)/shard_map/all_to_all | solution.py:98
Sparse Core Ops, SparseCore 0:
  10.1 59.3 all-gather.1
  213.0 136.7 reduce-scatter.1

commit v6 on v5

--- a/solution.py
+++ b/solution.py
@@ -84,39 +84,34 @@
     out_part = jnp.dot(activation, contract_local, preferred_element_type=jnp.float32).astype(
         jnp.bfloat16
     )
-    grad_activation = transposed_product(recv_g.reshape(slot_count, full_width), contract_local)
+    grad_activation = transposed_product(recv_g, contract_local)
     grad_hidden = (grad_activation * derivative).astype(jnp.bfloat16)
     back_part = transposed_product(grad_hidden, expand_local).astype(jnp.bfloat16)
-    out_part, back_part = lax.optimization_barrier((out_part, back_part))
-    out_rows = lax.psum_scatter(out_part, BLOCK_AXES, scatter_dimension=1, tiled=True)
-    block_count = full_width // width_share
-    back_blocks = lax.all_to_all(
-        back_part.reshape(slot_count, block_count, width_share), BLOCK_AXES, 1, 1, tiled=True
+    send_parts = jnp.concatenate(
+        [out_part.reshape(experts, chunk_rows, lane), back_part.reshape(experts, chunk_rows, lane)],
+        axis=1,
     )
-    out_rows, back_blocks = lax.optimization_barrier((out_rows, back_blocks))
-    back_rows = jnp.sum(back_blocks.astype(jnp.float32), axis=1).astype(jnp.bfloat16)
-    returned_out = lax.all_to_all(
-        out_rows.reshape(experts, capacity, width_share), "expert", split_axis=0, concat_axis=0,
+    recv_parts = lax.all_to_all(send_parts, "expert", split_axis=0, concat_axis=0, tiled=True)
+    returned_out = recv_parts[:, :chunk_rows].reshape(slot_count, full_width)
+    returned_back = recv_parts[:, chunk_rows:].reshape(slot_count, full_width)
+    out_pairs = jnp.dot(
+        placement_matrix, returned_out, preferred_element_type=jnp.float32
+    ).reshape(tok_rows, 2, full_width)
+    back_pairs = jnp.dot(
+        placement_matrix, returned_back, preferred_element_type=jnp.float32
+    ).reshape(tok_rows, 2, full_width)
+    combined_part = jnp.sum(gate_values[:, :, None] * out_pairs, axis=1)
+    input_part = back_pairs[:, 0, :] + back_pairs[:, 1, :]
+    partial_dots = jnp.sum(whole_cot[:, None, :].astype(jnp.float32) * out_pairs, axis=2)
+    reduced = lax.psum_scatter(
+        jnp.stack([combined_part, input_part]).astype(jnp.bfloat16),
+        BLOCK_AXES,
+        scatter_dimension=2,
         tiled=True,
     )
-    out_pairs = jnp.dot(
-        placement_matrix,
-        returned_out.reshape(slot_count, width_share),
-        preferred_element_type=jnp.float32,
-    ).reshape(tok_rows, 2, width_share)
-    combined = jnp.sum(gate_values[:, :, None] * out_pairs, axis=1).astype(jnp.bfloat16)
-    partial_dots = jnp.sum(cotangent[:, None, :].astype(jnp.float32) * out_pairs, axis=2)
     gate_grad = lax.psum(partial_dots, BLOCK_AXES)
-    returned_back = lax.all_to_all(
-        back_rows.reshape(experts, capacity, width_share), "expert", split_axis=0, concat_axis=0,
-        tiled=True,
-    )
-    back_pairs = jnp.dot(
-        placement_matrix,
-        returned_back.reshape(slot_count, width_share),
-        preferred_element_type=jnp.float32,
-    ).reshape(tok_rows, 2, width_share)
-    input_grad = (back_pairs[:, 0, :] + back_pairs[:, 1, :]).astype(jnp.bfloat16)
+    combined = reduced[0]
+    input_grad = reduced[1]
     return (combined, input_grad, gate_grad)
 
 

time: 424 us -> 388 us (0.915)
  waiting for transfers between devices: 218 us -> 173 us
  local copies, waits for them, and re-layouts: 32.8 us -> 50.3 us
  starting transfers between devices: 20.3 us -> 5.98 us
    reduce_scatter x1, waiting for transfers between devices: 140 us -> 43.5 us  [per_device(): lax.psum_scatter(jnp.stack([combined_part, input_part]).astype(jnp.bfloat...]
    all_to_all x3 -> x1, waiting for transfers between devices: 20.2 us -> 72.3 us  [per_device(): lax.all_to_all(send_parts, 'expert', split_axis=0, concat_axis=0, tiled=T...]
    all_to_all x3 -> x1, starting transfers between devices: 20.2 us -> 5.9 us  [per_device(): lax.all_to_all(send_parts, 'expert', split_axis=0, concat_axis=0, tiled=T...]
    reshape x5 -> x4, local copies, waits for them, and re-layouts: 4.34 us -> 14.9 us  [the longest x1 3.77 us: per_device(): out_part.reshape(experts, chunk_rows, lane)]
  transfers between devices with their start and end apart: 5 -> 3, of which waited for: 4 -> 3; matrix products, arithmetic and copies ran while one was open for 1% -> 1% of each run, Pallas kernels for 0% -> 0%
where the time goes in v6:
time: 388 us; the launch traced here: 384 us
  waiting for transfers between devices  173 us (45%)
  blocking collectives  109 us (28%)
  local copies, waits for them, and re-layouts  50.3 us (13%)
  matrix products  20.7 us (5%)
  between operations  14.2 us (4%)
  other arithmetic  11.1 us (3%)
  starting transfers between devices  5.98 us (2%)
    all_to_all x1, blocking collectives, per_device(): lax.all_to_all(send_xg, 'expert', split_axis=0, concat_axis=0, tiled=True)  85.5 us
    all_to_all x1, waiting for transfers between devices, per_device(): lax.all_to_all(send_parts, 'expert', split_axis=0, concat_axis=0, tiled=T...  72.3 us
    all_gather x1, waiting for transfers between devices, per_device(): whole_stacked = lax.all_gather(stacked, BLOCK_AXES, axis=2, tiled=True)  57.6 us
    reduce_scatter x1, waiting for transfers between devices, per_device(): lax.psum_scatter(jnp.stack([combined_part, input_part]).astype(jnp.bfloat...  43.5 us
    psum x1, blocking collectives, per_device(): gate_grad = lax.psum(partial_dots, BLOCK_AXES)  23.1 us
  transfers between devices with their start and end apart: 3, of which 3 were waited for; matrix products, arithmetic and copies ran while one was open for 1% of the time, Pallas kernels for 0%

profile of v6, /device:TPU:1, one launch (start us, length us, event | category | flops | bytes accessed | tf_op | source)
XLA Modules:
  0.0 384.3 jit_solution(2455368969006133258)
XLA Ops:
  7.2 0.0 copy-start
  7.2 0.0 all-gather.2.cloned.1.call-start
  7.2 1.7 pad_maximum_fusion.3
  8.9 0.0 all-gather.2.cloned.1.call-update
  8.9 0.8 copy.17
  9.7 0.1 eq.65
  9.8 0.1 eq.69
  10.0 0.6 reduce-window.6
  10.6 0.2 slice_reduce_fusion
  10.8 0.8 copy.21
  11.6 0.1 mul.110
  11.8 0.1 fusion.52
  11.9 57.6 %all-gather.2.cloned.1.call-done = bf16[128,2,2048]{2,0,1:T(8,128)(2,1)} async-done(((bf16[128,2,256]{2,0,1:T(8,128)(2,1)}), bf16[128,2,2048]{2,0,1:T(8,128)(2,1)}) %all-gather.2.cloned.1.call-update) | async-done | bytes 1048592 | tf_op jit(solution)/shard_map/all_gather | solution.py:57
  69.5 1.3 slice_bitcast_fusion.1
  70.9 1.6 broadcast_in_dim.5
  72.5 2.2 reshape.117
  74.7 3.1 convolution_convert_fusion.3
  77.8 3.8 reshape_reshape.6
  81.6 2.5 mul.114.clone
  84.1 3.7 mul.115
  87.8 3.4 convolution_convert_fusion.2
  91.2 3.8 reshape_reshape.7
  95.0 2.2 pad_maximum_fusion
  97.1 85.5 %all_to_all.10 = bf16[64,192,128]{2,1,0:T(8,128)(2,1)S(1)} all-to-all(bf16[64,192,128]{2,1,0:T(8,128)(2,1)S(1)} %pad_maximum_fusion), channel_id=1, replica_groups=mesh['sec'=2,'section'=4,'expert'=64] {'expert'}, dimensions={0} | all-to-all | bytes 6291456 | tf_op jit(solution)/shard_map/all_to_all | solution.py:76
  182.7 1.9 fusion.64
  184.5 3.7 reshape.118
  188.2 3.0 fusion.4
  191.3 0.0 copy-start.4
  191.3 0.9 copy-done.4
  192.2 0.0 copy-done
  192.2 2.2 convolution_convert_fusion.1
  194.4 3.8 reshape.119
  198.1 3.7 reshape.120
  201.8 5.7 %convolution_convert_fusion = bf16[384,2048]{1,0:T(8,128)(2,1)} fusion(bf16[1,2048,512]{2,1,0:T(8,128)(2,1)} %param.10, bf16[384,2048]{1,0:T(8,128)(2,1)} %reshape.120, bf16[1,512,2048]{2,1,0:T(8,128)(2,1)S(1)} %copy-done, f32[384,512]{1,0:T(8,128)} %copy-done.4), kind=kOutput, calls=%fused_computation.2 | convolution fusion | flops 1615134720 | bytes 8126464 | tf_op jit(solution)/shard_map/dot_general | solution.py:30
  207.5 3.7 reshape.121
  211.2 3.9 %pad_maximum_fusion.1 = bf16[64,192,128]{2,1,0:T(8,128)(2,1)} fusion(bf16[64,96,128]{2,1,0:T(8,128)(2,1)} %reshape.121, bf16[64,96,128]{2,1,0:T(8,128)(2,1)} %reshape.119), kind=kLoop, calls=%fused_computation.1 | loop fusion | flops 6291456 | bytes 6291456 | tf_op jit(solution)/shard_map/concatenate | solution.py:90
  215.1 0.0 copy-start.2
  215.1 5.9 %all-to-all-start.1 = ((bf16[64,192,128]{2,1,0:T(8,128)(2,1)}), bf16[64,192,128]{2,1,0:T(8,128)(2,1)}, u32[]{:S(2)}, u32[]{:S(2)}) async-start(bf16[64,192,128]{2,1,0:T(8,128)(2,1)} %pad_maximum_fusion.1), calls=%async_computation.1 | async-start | bytes 6291456 | tf_op jit(solution)/shard_map/all_to_all | solution.py:94
  221.0 0.0 reduce-scatter.2.cloned.1.call-start
  221.1 0.1 reduce_sum.30
  221.2 0.1 copy.20
  221.3 0.0 copy-done.2
  221.3 72.3 %all-to-all-done.1 = bf16[64,192,128]{2,1,0:T(8,128)(2,1)} async-done(((bf16[64,192,128]{2,1,0:T(8,128)(2,1)}), bf16[64,192,128]{2,1,0:T(8,128)(2,1)}, u32[]{:S(2)}, u32[]{:S(2)}) %all-to-all-start.1) | async-done | bytes 3145760 | tf_op jit(solution)/shard_map/all_to_all | solution.py:94
  293.6 3.8 fusion.63
  297.4 3.7 reshape.125
  301.1 0.0 copy-start.3
  301.1 3.7 reshape.126
  304.8 0.0 copy-done.3
  304.8 0.0 copy-start.1
  304.8 2.5 multiply_reduce_fusion
  307.3 0.0 copy-done.1
  307.3 0.8 fusion.42
  308.1 0.1 fusion.29
  308.2 1.1 pad_maximum_fusion.2
  309.3 0.0 reduce-scatter.2.cloned.1.call-update
  309.3 23.1 %psum.7 = f32[128,2]{0,1:T(2,128)} all-reduce(f32[128,2]{0,1:T(2,128)S(1)} %get-tuple-element.3), channel_id=1, replica_groups=mesh['sec'=2,'section'=4,'expert'=64] {'sec','section'}, use_global_device_ids=true, to_apply=%region_6.7 | all-reduce | flops 256 | bytes 2048 | tf_op jit(solution)/shard_map/psum | solution.py:112
  332.4 43.5 %reduce-scatter.2.cloned.1.call-done = bf16[2,128,256]{2,1,0:T(8,128)(2,1)} async-done(((bf16[2,128,2048]{2,1,0:T(8,128)(2,1)}), bf16[2,128,256]{2,1,0:T(8,128)(2,1)}) %reduce-scatter.2.cloned.1.call-update) | async-done | bytes 131088 | tf_op jit(solution)/shard_map/reduce_scatter | solution.py:106
  375.9 1.5 slice_bitcast_fusion.2
  (5 shorter events, 0.1 us)
Async XLA Ops:
  7.2 185.0 %copy-start = (bf16[1,512,2048]{2,1,0:T(8,128)(2,1)S(1)}, bf16[1,512,2048]{2,1,0:T(8,128)(2,1)}, u32[]{:S(2)}) copy-start(bf16[1,512,2048]{2,1,0:T(8,128)(2,1)} %param.11) | copy-start | bytes 6291460
  7.2 62.3 %all-gather.2.cloned.1.call-start = ((), (), s32[]{:S(2)}) async-start(), calls=%async_computation.3 | async-start | bytes 1179648 | tf_op jit(solution)/shard_map/all_gather | solution.py:57
  191.3 0.9 copy-start.4
  215.1 6.2 %copy-start.2 = (s32[128,2]{0,1:T(2,128)S(1)}, s32[128,2]{0,1:T(2,128)}, u32[]{:S(2)}) copy-start(s32[128,2]{0,1:T(2,128)} %param.8) | copy-start | bytes 3076
  215.1 78.4 %all-to-all-start.1 = ((bf16[64,192,128]{2,1,0:T(8,128)(2,1)}), bf16[64,192,128]{2,1,0:T(8,128)(2,1)}, u32[]{:S(2)}, u32[]{:S(2)}) async-start(bf16[64,192,128]{2,1,0:T(8,128)(2,1)} %pad_maximum_fusion.1), calls=%async_computation.1 | async-start | bytes 6291456 | tf_op jit(solution)/shard_map/all_to_all | solution.py:94
  221.0 154.8 %reduce-scatter.2.cloned.1.call-start = ((), (), s32[]{:S(2)}) async-start(), calls=%async_computation.4 | async-start | bytes 1179648 | tf_op jit(solution)/shard_map/reduce_scatter | solution.py:106
  301.1 3.7 copy-start.3
  304.8 2.5 copy-start.1
Sparse Core Ops, SparseCore 0:
  10.1 59.3 all-gather.1
  309.4 66.4 reduce-scatter.1

commit v7 on v6

--- a/solution.py
+++ b/solution.py
@@ -48,63 +48,72 @@
         positions[:, None] == jnp.arange(slot_count, dtype=jnp.int32)[None, :]
     ).astype(jnp.bfloat16)
 
-    def to_slots(pairs):
-        return jnp.dot(placement_matrix.T, pairs, preferred_element_type=jnp.float32).astype(
-            jnp.bfloat16
-        )
+    lane = 128
+    groups = full_width // lane
+    chunk_rows = capacity * groups
+    pair_to_slot = placement_matrix
+    token_to_slot = jnp.sum(
+        placement_matrix.reshape(tok_rows, 2, slot_count), axis=1, dtype=jnp.float32
+    ).astype(jnp.bfloat16)
+
+    def gather_rows(selector, rows):
+        return lax.dot_general(
+            selector, rows, (((0,), (0,)), ((), ())), preferred_element_type=jnp.float32
+        ).astype(jnp.bfloat16)
 
     stacked = jnp.stack([tokens, cotangent], axis=1)
     whole_stacked = lax.all_gather(stacked, BLOCK_AXES, axis=2, tiled=True)
-    whole_tokens = whole_stacked[:, 0, :]
-    whole_cot = whole_stacked[:, 1, :]
-    whole_grad = (gate_values[:, :, None] * whole_cot[:, None, :].astype(jnp.float32)).astype(
-        jnp.bfloat16
-    )
-    pair_tokens = jnp.broadcast_to(whole_tokens[:, None, :], (tok_rows, 2, full_width)).reshape(
-        2 * tok_rows, full_width
-    )
-    send_x = to_slots(pair_tokens).reshape(experts, capacity, full_width)
-    send_g = to_slots(whole_grad.reshape(2 * tok_rows, full_width)).reshape(
-        experts, capacity, full_width
-    )
-    lane = 128
-    chunk_rows = capacity * full_width // lane
+    whole_tokens = whole_stacked[:, 0, :].reshape(tok_rows, groups, lane)
+    whole_cot = whole_stacked[:, 1, :].reshape(tok_rows, groups, lane)
+    whole_grad = (
+        gate_values[:, :, None, None] * whole_cot[:, None, :, :].astype(jnp.float32)
+    ).astype(jnp.bfloat16)
+    send_x = gather_rows(token_to_slot, whole_tokens)
+    send_g = gather_rows(pair_to_slot, whole_grad.reshape(2 * tok_rows, groups, lane))
     send_xg = jnp.concatenate(
         [send_x.reshape(experts, chunk_rows, lane), send_g.reshape(experts, chunk_rows, lane)],
         axis=1,
     )
     recv_xg = lax.all_to_all(send_xg, "expert", split_axis=0, concat_axis=0, tiled=True)
-    recv_x = recv_xg[:, :chunk_rows].reshape(slot_count, full_width)
-    recv_g = recv_xg[:, chunk_rows:].reshape(slot_count, full_width)
-    hidden = jnp.dot(
-        recv_x.reshape(slot_count, full_width), expand_local, preferred_element_type=jnp.float32
+    recv_x = recv_xg[:, :chunk_rows].reshape(slot_count, groups, lane)
+    recv_g = recv_xg[:, chunk_rows:].reshape(slot_count, groups, lane)
+    expand_3d = expand_local.reshape(groups, lane, -1)
+    contract_3d = contract_local.reshape(-1, groups, lane)
+    hidden = lax.dot_general(
+        recv_x, expand_3d, (((1, 2), (0, 1)), ((), ())), preferred_element_type=jnp.float32
     )
     activation, derivative = gelu_parts(hidden)
     activation = activation.astype(jnp.bfloat16)
-    out_part = jnp.dot(activation, contract_local, preferred_element_type=jnp.float32).astype(
-        jnp.bfloat16
+    out_part = lax.dot_general(
+        activation, contract_3d, (((1,), (0,)), ((), ())), preferred_element_type=jnp.float32
+    ).astype(jnp.bfloat16)
+    grad_activation = lax.dot_general(
+        recv_g, contract_3d, (((1, 2), (1, 2)), ((), ())), preferred_element_type=jnp.float32
     )
-    grad_activation = transposed_product(recv_g, contract_local)
     grad_hidden = (grad_activation * derivative).astype(jnp.bfloat16)
-    back_part = transposed_product(grad_hidden, expand_local).astype(jnp.bfloat16)
+    back_part = lax.dot_general(
+        grad_hidden, expand_3d, (((1,), (2,)), ((), ())), preferred_element_type=jnp.float32
+    ).astype(jnp.bfloat16)
     send_parts = jnp.concatenate(
         [out_part.reshape(experts, chunk_rows, lane), back_part.reshape(experts, chunk_rows, lane)],
         axis=1,
     )
     recv_parts = lax.all_to_all(send_parts, "expert", split_axis=0, concat_axis=0, tiled=True)
-    returned_out = recv_parts[:, :chunk_rows].reshape(slot_count, full_width)
-    returned_back = recv_parts[:, chunk_rows:].reshape(slot_count, full_width)
-    out_pairs = jnp.dot(
-        placement_matrix, returned_out, preferred_element_type=jnp.float32
-    ).reshape(tok_rows, 2, full_width)
-    back_pairs = jnp.dot(
-        placement_matrix, returned_back, preferred_element_type=jnp.float32
-    ).reshape(tok_rows, 2, full_width)
-    combined_part = jnp.sum(gate_values[:, :, None] * out_pairs, axis=1)
-    input_part = back_pairs[:, 0, :] + back_pairs[:, 1, :]
-    partial_dots = jnp.sum(whole_cot[:, None, :].astype(jnp.float32) * out_pairs, axis=2)
+    returned_out = recv_parts[:, :chunk_rows].reshape(slot_count, groups, lane)
+    returned_back = recv_parts[:, chunk_rows:].reshape(slot_count, groups, lane)
+    out_pairs = lax.dot_general(
+        pair_to_slot, returned_out, (((1,), (0,)), ((), ())), preferred_element_type=jnp.float32
+    ).reshape(tok_rows, 2, groups, lane)
+    back_pairs = lax.dot_general(
+        pair_to_slot, returned_back, (((1,), (0,)), ((), ())), preferred_element_type=jnp.float32
+    ).reshape(tok_rows, 2, groups, lane)
+    combined_part = jnp.sum(gate_values[:, :, None, None] * out_pairs, axis=1)
+    input_part = back_pairs[:, 0] + back_pairs[:, 1]
+    partial_dots = jnp.sum(
+        whole_cot[:, None, :, :].astype(jnp.float32) * out_pairs, axis=(2, 3)
+    )
     reduced = lax.psum_scatter(
-        jnp.stack([combined_part, input_part]).astype(jnp.bfloat16),
+        jnp.stack([combined_part, input_part]).astype(jnp.bfloat16).reshape(2, tok_rows, -1),
         BLOCK_AXES,
         scatter_dimension=2,
         tiled=True,

time: 388 us -> 348 us (0.90)
  blocking collectives: 109 us -> 31.6 us
  waiting for transfers between devices: 173 us -> 227 us
  local copies, waits for them, and re-layouts: 50.3 us -> 33.5 us
  starting transfers between devices: 5.98 us -> 14.8 us
  matrix products: 20.7 us -> 15.5 us
    all_to_all x1 -> x0, blocking collectives: 85.5 us -> none  [per_device(): lax.all_to_all(send_xg, 'expert', split_axis=0, concat_axis=0, tiled=True)]
    all_to_all x0 -> x1, waiting for transfers between devices: none -> 69.2 us  [per_device(): lax.all_to_all(send_xg, 'expert', split_axis=0, concat_axis=0, tiled=True)]
    reshape x7 -> x2, local copies, waits for them, and re-layouts: 24.5 us -> 5.82 us  [the longest x1 2.95 us: per_device(): returned_out = recv_parts[:, :chunk_rows].reshape(slot_count, groups, lane)]
    all_to_all x0 -> x1, starting transfers between devices: none -> 8.82 us  [per_device(): lax.all_to_all(send_xg, 'expert', split_axis=0, concat_axis=0, tiled=True)]
    all_gather x1, waiting for transfers between devices: 57.6 us -> 48.9 us  [per_device(): whole_stacked = lax.all_gather(stacked, BLOCK_AXES, axis=2, tiled=True)]
    psum x1, blocking collectives: 23.1 us -> 31.6 us  [per_device(): gate_grad = lax.psum(partial_dots, BLOCK_AXES)]
    unnamed x12 -> x18, local copies, waits for them, and re-layouts: 2.49 us -> 9.16 us
    reduce_scatter x1, waiting for transfers between devices: 43.5 us -> 37.1 us  [per_device(): lax.psum_scatter(jnp.stack([combined_part, input_part]).astype(jnp.bfloat...]
  transfers between devices with their start and end apart: 3 -> 4, of which waited for: 3 -> 4; matrix products, arithmetic and copies ran while one was open for 1% -> 2% of each run, Pallas kernels for 0% -> 0%
where the time goes in v7:
time: 348 us; the launch traced here: 347 us
  waiting for transfers between devices  227 us (65%)
  local copies, waits for them, and re-layouts  33.5 us (10%)
  blocking collectives  31.6 us (9%)
  matrix products  15.5 us (4%)
  starting transfers between devices  14.8 us (4%)
  between operations  14.2 us (4%)
  other arithmetic  11.3 us (3%)
    all_to_all x1, waiting for transfers between devices, per_device(): lax.all_to_all(send_parts, 'expert', split_axis=0, concat_axis=0, tiled=T...  71.4 us
    all_to_all x1, waiting for transfers between devices, per_device(): lax.all_to_all(send_xg, 'expert', split_axis=0, concat_axis=0, tiled=True)  69.2 us
    all_gather x1, waiting for transfers between devices, per_device(): whole_stacked = lax.all_gather(stacked, BLOCK_AXES, axis=2, tiled=True)  48.9 us
    reduce_scatter x1, waiting for transfers between devices, per_device(): lax.psum_scatter(jnp.stack([combined_part, input_part]).astype(jnp.bfloat...  37.1 us
    psum x1, blocking collectives, per_device(): gate_grad = lax.psum(partial_dots, BLOCK_AXES)  31.6 us
    unnamed x18, local copies, waits for them, and re-layouts  9.16 us
    all_to_all x1, starting transfers between devices, per_device(): lax.all_to_all(send_xg, 'expert', split_axis=0, concat_axis=0, tiled=True)  8.82 us
  transfers between devices with their start and end apart: 4, of which 4 were waited for; matrix products, arithmetic and copies ran while one was open for 2% of the time, Pallas kernels for 0%

profile of v7, /device:TPU:1, one launch (start us, length us, event | category | flops | bytes accessed | tf_op | source)
XLA Modules:
  0.0 347.5 jit_solution(3413153506665292146)
XLA Ops:
  7.2 0.0 copy-start
  7.2 0.0 all-gather.2.cloned.1.call-start
  7.2 1.1 copy.111
  8.3 1.0 copy.112
  9.3 0.7 pad_maximum_fusion.3
  9.9 0.0 all-gather.2.cloned.1.call-update
  10.0 0.8 copy.107
  10.8 0.1 eq.76
  10.9 0.1 eq.72
  11.1 0.6 reduce-window.6
  11.7 0.2 slice_reduce_fusion
  11.9 0.8 copy.116
  12.7 0.1 mul.105
  12.8 0.1 fusion.80
  12.9 0.1 reduce_sum.42
  13.1 0.1 copy.110
  13.1 0.7 multiply_add_fusion.2
  13.8 0.1 fusion.73
  14.0 48.9 %all-gather.2.cloned.1.call-done = bf16[128,2,2048]{0,2,1:T(8,128)(2,1)} async-done(((bf16[128,2,256]{0,2,1:T(8,128)(2,1)}), bf16[128,2,2048]{0,2,1:T(8,128)(2,1)}) %all-gather.2.cloned.1.call-update) | async-done | bytes 1048592 | tf_op jit(solution)/shard_map/all_gather | solution.py:65
  62.8 1.3 fusion.93
  64.1 1.3 copy.134
  65.5 1.6 fusion
  67.0 0.6 convolution_convert_fusion.2
  67.6 1.0 copy.119
  68.7 0.6 convolution_convert_fusion.1
  69.3 1.0 copy.115
  70.3 2.1 pad_maximum_fusion
  72.4 8.8 %all-to-all-start = ((bf16[64,192,128]{2,1,0:T(8,128)(2,1)}), bf16[64,192,128]{2,1,0:T(8,128)(2,1)}, u32[]{:S(2)}, u32[]{:S(2)}) async-start(bf16[64,192,128]{2,1,0:T(8,128)(2,1)} %pad_maximum_fusion), calls=%async_computation | async-start | bytes 6291456 | tf_op jit(solution)/shard_map/all_to_all | solution.py:77
  81.2 3.6 %copy.136 = bf16[64,8,16,128]{3,2,1,0:T(8,128)(2,1)} copy(bf16[64,8,16,128]{3,1,2,0:T(8,128)(2,1)} %bitcast.102) | data formatting | bytes 4194304
  84.8 69.2 %all-to-all-done = bf16[64,192,128]{2,1,0:T(8,128)(2,1)} async-done(((bf16[64,192,128]{2,1,0:T(8,128)(2,1)}), bf16[64,192,128]{2,1,0:T(8,128)(2,1)}, u32[]{:S(2)}, u32[]{:S(2)}) %all-to-all-start) | async-done | bytes 3145760 | tf_op jit(solution)/shard_map/all_to_all | solution.py:77
  154.0 3.2 fusion.92
  157.2 0.0 copy-done
  157.2 0.0 copy-start.1
  157.2 1.0 fusion.15
  158.2 0.0 copy-start.5
  158.2 0.6 copy-done.1
  158.8 2.3 fusion.5
  161.1 0.0 copy-done.5
  161.1 5.6 %convolution_convert_fusion = bf16[384,16,128]{2,0,1:T(8,128)(2,1)} fusion(bf16[16,128,512]{2,1,0:T(8,128)(2,1)S(1)} %bitcast.92, bf16[512,16,128]{2,1,0:T(8,128)(2,1)} %bitcast.103, bf16[384,16,128]{2,1,0:T(8,128)(2,1)} %bitcast.106, f32[384,512]{1,0:T(8,128)} %copy-done.5), kind=kOutput, calls=%fused_computation.11 | convolution fusion | flops 1615134720 | bytes 8126464 | tf_op jit(solution)/shard_map/dot_general | solution.py:94
  166.7 0.0 copy-start.2
  166.7 2.5 copy.125
  169.3 0.0 copy-done.2
  169.3 1.0 copy.122
  170.3 2.1 pad_maximum_fusion.1
  172.4 5.9 %all-to-all-start.1 = ((bf16[64,192,128]{2,1,0:T(8,128)(2,1)}), bf16[64,192,128]{2,1,0:T(8,128)(2,1)}, u32[]{:S(2)}, u32[]{:S(2)}) async-start(bf16[64,192,128]{2,1,0:T(8,128)(2,1)} %pad_maximum_fusion.1), calls=%async_computation.1 | async-start | bytes 6291456 | tf_op jit(solution)/shard_map/all_to_all | solution.py:101
  178.3 0.0 reduce-scatter.2.cloned.1.call-start
  178.4 1.1 convert.12
  179.5 71.4 %all-to-all-done.1 = bf16[64,192,128]{2,1,0:T(8,128)(2,1)} async-done(((bf16[64,192,128]{2,1,0:T(8,128)(2,1)}), bf16[64,192,128]{2,1,0:T(8,128)(2,1)}, u32[]{:S(2)}, u32[]{:S(2)}) %all-to-all-start.1) | async-done | bytes 3145760 | tf_op jit(solution)/shard_map/all_to_all | solution.py:101
  250.9 3.8 %fusion.91 = (bf16[64,96,128]{2,1,0:T(8,128)(2,1)}, bf16[64,96,128]{2,1,0:T(8,128)(2,1)}) fusion(bf16[64,192,128]{2,1,0:T(8,128)(2,1)} %all-to-all-done.1), kind=kLoop, calls=%fused_computation.88 | loop fusion | bytes 6291456 | tf_op jit(solution)/shard_map/slice | solution.py:102
  254.6 0.0 copy-start.3
  254.7 3.0 copy.126
  257.6 0.0 copy-done.3
  257.6 0.0 copy-done.4
  257.6 3.2 multiply_reduce_fusion
  260.8 1.2 copy.128
  262.0 2.9 copy.127
  264.9 2.2 fusion.8
  267.1 0.1 fusion.38
  267.2 1.0 copy.129
  268.3 2.1 pad_maximum_fusion.2
  270.4 0.0 reduce-scatter.2.cloned.1.call-update
  270.4 31.6 %psum.7 = f32[128,2]{0,1:T(2,128)} all-reduce(f32[128,2]{0,1:T(2,128)S(1)} %get-tuple-element.3), channel_id=1, replica_groups=mesh['sec'=2,'section'=4,'expert'=64] {'sec','section'}, use_global_device_ids=true, to_apply=%region_7.8 | all-reduce | flops 256 | bytes 2048 | tf_op jit(solution)/shard_map/psum | solution.py:121
  302.0 37.1 %reduce-scatter.2.cloned.1.call-done = bf16[2,128,256]{2,1,0:T(8,128)(2,1)} async-done(((bf16[2,128,2048]{2,1,0:T(8,128)(2,1)}), bf16[2,128,256]{2,1,0:T(8,128)(2,1)}) %reduce-scatter.2.cloned.1.call-update) | async-done | bytes 131088 | tf_op jit(solution)/shard_map/reduce_scatter | solution.py:115
  339.1 1.5 slice_bitcast_fusion
  (5 shorter events, 0.1 us)
Async XLA Ops:
  7.2 150.0 %copy-start = (bf16[1,2048,512]{2,1,0:T(8,128)(2,1)S(1)}, bf16[1,2048,512]{2,1,0:T(8,128)(2,1)}, u32[]{:S(2)}) copy-start(bf16[1,2048,512]{2,1,0:T(8,128)(2,1)} %param.10) | copy-start | bytes 6291460
  7.2 55.7 %all-gather.2.cloned.1.call-start = ((), (), s32[]{:S(2)}) async-start(), calls=%async_computation.3 | async-start | bytes 1179648 | tf_op jit(solution)/shard_map/all_gather | solution.py:65
  72.4 81.6 %all-to-all-start = ((bf16[64,192,128]{2,1,0:T(8,128)(2,1)}), bf16[64,192,128]{2,1,0:T(8,128)(2,1)}, u32[]{:S(2)}, u32[]{:S(2)}) async-start(bf16[64,192,128]{2,1,0:T(8,128)(2,1)} %pad_maximum_fusion), calls=%async_computation | async-start | bytes 6291456 | tf_op jit(solution)/shard_map/all_to_all | solution.py:77
  157.2 1.6 copy-start.1
  158.2 2.9 copy-start.5
  166.7 2.5 copy-start.2
  172.4 78.5 %all-to-all-start.1 = ((bf16[64,192,128]{2,1,0:T(8,128)(2,1)}), bf16[64,192,128]{2,1,0:T(8,128)(2,1)}, u32[]{:S(2)}, u32[]{:S(2)}) async-start(bf16[64,192,128]{2,1,0:T(8,128)(2,1)} %pad_maximum_fusion.1), calls=%async_computation.1 | async-start | bytes 6291456 | tf_op jit(solution)/shard_map/all_to_all | solution.py:101
  178.3 160.8 %reduce-scatter.2.cloned.1.call-start = ((), (), s32[]{:S(2)}) async-start(), calls=%async_computation.4 | async-start | bytes 1179648 | tf_op jit(solution)/shard_map/reduce_scatter | solution.py:115
  254.6 3.0 copy-start.3
  254.6 3.0 copy-start.4
Sparse Core Ops, SparseCore 0:
  10.1 52.6 all-gather.1
  270.5 68.5 reduce-scatter.1

commit v8 on v7

--- a/solution.py
+++ b/solution.py
@@ -101,16 +101,28 @@
     recv_parts = lax.all_to_all(send_parts, "expert", split_axis=0, concat_axis=0, tiled=True)
     returned_out = recv_parts[:, :chunk_rows].reshape(slot_count, groups, lane)
     returned_back = recv_parts[:, chunk_rows:].reshape(slot_count, groups, lane)
-    out_pairs = lax.dot_general(
-        pair_to_slot, returned_out, (((1,), (0,)), ((), ())), preferred_element_type=jnp.float32
-    ).reshape(tok_rows, 2, groups, lane)
-    back_pairs = lax.dot_general(
-        pair_to_slot, returned_back, (((1,), (0,)), ((), ())), preferred_element_type=jnp.float32
-    ).reshape(tok_rows, 2, groups, lane)
-    combined_part = jnp.sum(gate_values[:, :, None, None] * out_pairs, axis=1)
-    input_part = back_pairs[:, 0] + back_pairs[:, 1]
+    pair_gates = jnp.sum(
+        placement_matrix.reshape(tok_rows, 2, slot_count).astype(jnp.float32)
+        * gate_values[:, :, None],
+        axis=1,
+    )
+    gate_hi = pair_gates.astype(jnp.bfloat16)
+    gate_lo = (pair_gates - gate_hi.astype(jnp.float32)).astype(jnp.bfloat16)
+
+    def pick_rows(selector, rows):
+        return lax.dot_general(
+            selector, rows, (((1,), (0,)), ((), ())), preferred_element_type=jnp.float32
+        )
+
+    combined_part = pick_rows(gate_hi, returned_out) + pick_rows(gate_lo, returned_out)
+    input_part = pick_rows(token_to_slot, returned_back)
+    slot_dots = lax.dot_general(
+        whole_cot, returned_out, (((1, 2), (1, 2)), ((), ())), preferred_element_type=jnp.float32
+    )
     partial_dots = jnp.sum(
-        whole_cot[:, None, :, :].astype(jnp.float32) * out_pairs, axis=(2, 3)
+        placement_matrix.reshape(tok_rows, 2, slot_count).astype(jnp.float32)
+        * slot_dots[:, None, :],
+        axis=2,
     )
     reduced = lax.psum_scatter(
         jnp.stack([combined_part, input_part]).astype(jnp.bfloat16).reshape(2, tok_rows, -1),

time: 348 us -> 343 us (0.986); the launches traced: 347 us -> 339 us
  blocking collectives: 31.6 us -> 110 us
  waiting for transfers between devices: 227 us -> 153 us
  starting transfers between devices: 14.8 us -> 8.91 us
  other arithmetic: 11.3 us -> 7.23 us
    all_to_all x0 -> x1, blocking collectives: none -> 78.7 us  [per_device(): lax.all_to_all(send_parts, 'expert', split_axis=0, concat_axis=0, tiled=T...]
    all_to_all x1 -> x0, waiting for transfers between devices: 71.4 us -> none  [per_device(): lax.all_to_all(send_parts, 'expert', split_axis=0, concat_axis=0, tiled=T...]
    all_to_all x1 -> x0, starting transfers between devices: 5.92 us -> none  [per_device(): lax.all_to_all(send_parts, 'expert', split_axis=0, concat_axis=0, tiled=T...]
    unnamed x18 -> x19, local copies, waits for them, and re-layouts: 9.16 us -> 9.04 us
  transfers between devices with their start and end apart: 4 -> 3, of which waited for: 4 -> 3; matrix products, arithmetic and copies ran while one was open for 2% -> 2% of each run, Pallas kernels for 0% -> 0%
where the time goes in v8:
time: 343 us; the launch traced here: 339 us
  waiting for transfers between devices  153 us (45%)
  blocking collectives  110 us (32%)
  local copies, waits for them, and re-layouts  30.6 us (9%)
  matrix products  14.4 us (4%)
  between operations  14.3 us (4%)
  starting transfers between devices  8.91 us (3%)
  other arithmetic  7.23 us (2%)
    all_to_all x1, blocking collectives, per_device(): lax.all_to_all(send_parts, 'expert', split_axis=0, concat_axis=0, tiled=T...  78.7 us
    all_to_all x1, waiting for transfers between devices, per_device(): lax.all_to_all(send_xg, 'expert', split_axis=0, concat_axis=0, tiled=True)  69.2 us
    all_gather x1, waiting for transfers between devices, per_device(): whole_stacked = lax.all_gather(stacked, BLOCK_AXES, axis=2, tiled=True)  48.9 us
    reduce_scatter x1, waiting for transfers between devices, per_device(): lax.psum_scatter(jnp.stack([combined_part, input_part]).astype(jnp.bfloat...  35.3 us
    psum x1, blocking collectives, per_device(): gate_grad = lax.psum(partial_dots, BLOCK_AXES)  31.4 us
    unnamed x19, local copies, waits for them, and re-layouts  9.04 us
    all_to_all x1, starting transfers between devices, per_device(): lax.all_to_all(send_xg, 'expert', split_axis=0, concat_axis=0, tiled=True)  8.65 us
  transfers between devices with their start and end apart: 3, of which 3 were waited for; matrix products, arithmetic and copies ran while one was open for 2% of the time, Pallas kernels for 0%

profile of v8, /device:TPU:1, one launch (start us, length us, event | category | flops | bytes accessed | tf_op | source)
XLA Modules:
  0.0 338.9 jit_solution(18370474839577847607)
XLA Ops:
  7.2 0.0 copy-start
  7.2 0.0 all-gather.2.cloned.1.call-start
  7.2 1.1 copy.89
  8.3 1.0 copy.90
  9.3 0.7 pad_maximum_fusion.3
  9.9 0.0 all-gather.2.cloned.1.call-update
  10.0 0.8 copy.85
  10.8 0.1 eq.45
  10.9 0.1 eq.49
  11.1 0.6 reduce-window.6
  11.7 0.2 slice_reduce_fusion
  11.9 0.1 fusion.75
  12.0 0.1 reduce_sum.42
  12.2 0.1 copy.88
  12.2 0.8 copy.94
  13.0 0.1 mul.108
  13.2 0.7 multiply_add_fusion.2
  13.9 0.1 fusion.69
  14.0 48.9 %all-gather.2.cloned.1.call-done = bf16[128,2,2048]{0,2,1:T(8,128)(2,1)} async-done(((bf16[128,2,256]{0,2,1:T(8,128)(2,1)}), bf16[128,2,2048]{0,2,1:T(8,128)(2,1)}) %all-gather.2.cloned.1.call-update) | async-done | bytes 1048592 | tf_op jit(solution)/shard_map/all_gather | solution.py:65
  62.8 1.3 fusion.91
  64.1 0.6 convolution_convert_fusion.2
  64.7 2.2 copy.93
  66.9 1.2 copy.95
  68.1 1.9 mul.110
  70.0 0.7 convolution_convert_fusion.3
  70.7 0.0 copy-start.2
  70.7 1.0 copy.96
  71.8 0.4 copy-done.2
  72.1 2.1 pad_maximum_fusion
  74.2 8.7 %all-to-all-start = ((bf16[64,192,128]{2,1,0:T(8,128)(2,1)}), bf16[64,192,128]{2,1,0:T(8,128)(2,1)}, u32[]{:S(2)}, u32[]{:S(2)}) async-start(bf16[64,192,128]{2,1,0:T(8,128)(2,1)} %pad_maximum_fusion), calls=%async_computation | async-start | bytes 6291456 | tf_op jit(solution)/shard_map/all_to_all | solution.py:77
  82.9 0.2 reduce-scatter.2.cloned.1.call-start
  83.1 3.6 %copy.113 = bf16[64,8,16,128]{3,2,1,0:T(8,128)(2,1)} copy(bf16[64,8,16,128]{3,1,2,0:T(8,128)(2,1)} %bitcast.106) | data formatting | bytes 4194304
  86.7 69.2 %all-to-all-done = bf16[64,192,128]{2,1,0:T(8,128)(2,1)} async-done(((bf16[64,192,128]{2,1,0:T(8,128)(2,1)}), bf16[64,192,128]{2,1,0:T(8,128)(2,1)}, u32[]{:S(2)}, u32[]{:S(2)}) %all-to-all-start) | async-done | bytes 3145760 | tf_op jit(solution)/shard_map/all_to_all | solution.py:77
  155.8 3.2 fusion.90
  159.1 0.0 copy-done
  159.1 0.0 copy-start.4
  159.1 1.0 fusion.13
  160.0 0.6 copy-done.4
  160.7 2.3 fusion.5
  163.0 5.4 %convolution_convert_fusion.1 = bf16[384,16,128]{2,0,1:T(8,128)(2,1)} fusion(bf16[16,128,512]{2,1,0:T(8,128)(2,1)S(1)} %bitcast.91, bf16[512,16,128]{2,1,0:T(8,128)(2,1)} %bitcast.107, bf16[384,16,128]{2,1,0:T(8,128)(2,1)} %bitcast.110, f32[384,512]{1,0:T(8,128)S(1)} %fusion.13), kind=kOutput, calls=%fused_computation.10 | convolution fusion | flops 1615134720 | bytes 8126464 | tf_op jit(solution)/shard_map/dot_general | solution.py:94
  168.4 0.0 copy-start.5
  168.4 2.5 copy.99
  171.0 0.0 copy-done.5
  171.0 1.0 copy.102
  172.0 0.4 pad_maximum_fusion.1
  172.4 78.7 %all_to_all.10 = bf16[64,192,128]{2,1,0:T(8,128)(2,1)S(1)} all-to-all(bf16[64,192,128]{2,1,0:T(8,128)(2,1)S(1)} %pad_maximum_fusion.1), channel_id=1, replica_groups=mesh['sec'=2,'section'=4,'expert'=64] {'expert'}, dimensions={0} | all-to-all | bytes 6291456 | tf_op jit(solution)/shard_map/all_to_all | solution.py:101
  251.1 1.9 fusion.89
  253.0 2.8 copy.103
  255.8 2.0 convolution_bitcast_fusion
  257.8 0.0 copy-done.6
  257.9 0.2 fusion.56
  258.1 0.0 copy-done.1
  258.1 0.6 fusion.71
  258.7 0.0 copy-start.3
  258.7 0.6 fusion.78
  259.3 0.8 copy-done.3
  260.1 1.3 fusion
  261.4 0.1 add_convert_fusion
  261.5 0.2 copy.105
  261.7 2.1 pad_maximum_fusion.2
  263.8 0.0 reduce-scatter.2.cloned.1.call-update
  263.9 31.4 %psum.7 = f32[128,2]{0,1:T(2,128)} all-reduce(f32[128,2]{0,1:T(2,128)S(1)} %get-tuple-element.3), channel_id=1, replica_groups=mesh['sec'=2,'section'=4,'expert'=64] {'sec','section'}, use_global_device_ids=true, to_apply=%region_7.8 | all-reduce | flops 256 | bytes 2048 | tf_op jit(solution)/shard_map/psum | solution.py:133
  295.3 35.3 %reduce-scatter.2.cloned.1.call-done = bf16[2,128,256]{2,1,0:T(8,128)(2,1)} async-done(((bf16[2,128,2048]{2,1,0:T(8,128)(2,1)}), bf16[2,128,256]{2,1,0:T(8,128)(2,1)}) %reduce-scatter.2.cloned.1.call-update) | async-done | bytes 131088 | tf_op jit(solution)/shard_map/reduce_scatter | solution.py:127
  330.6 1.5 slice_bitcast_fusion
  (6 shorter events, 0.1 us)
Async XLA Ops:
  7.2 151.9 %copy-start = (bf16[1,2048,512]{2,1,0:T(8,128)(2,1)S(1)}, bf16[1,2048,512]{2,1,0:T(8,128)(2,1)}, u32[]{:S(2)}) copy-start(bf16[1,2048,512]{2,1,0:T(8,128)(2,1)} %param.10) | copy-start | bytes 6291460
  7.2 55.7 %all-gather.2.cloned.1.call-start = ((), (), s32[]{:S(2)}) async-start(), calls=%async_computation.3 | async-start | bytes 1179648 | tf_op jit(solution)/shard_map/all_gather | solution.py:65
  70.7 1.4 copy-start.2
  74.2 81.6 %all-to-all-start = ((bf16[64,192,128]{2,1,0:T(8,128)(2,1)}), bf16[64,192,128]{2,1,0:T(8,128)(2,1)}, u32[]{:S(2)}, u32[]{:S(2)}) async-start(bf16[64,192,128]{2,1,0:T(8,128)(2,1)} %pad_maximum_fusion), calls=%async_computation | async-start | bytes 6291456 | tf_op jit(solution)/shard_map/all_to_all | solution.py:77
  82.9 247.7 %reduce-scatter.2.cloned.1.call-start = ((), (), s32[]{:S(2)}) async-start(), calls=%async_computation.4 | async-start | bytes 1179648 | tf_op jit(solution)/shard_map/reduce_scatter | solution.py:127
  159.1 1.6 copy-start.4
  168.4 2.5 copy-start.5
  255.8 2.0 copy-start.6
  255.8 2.2 copy-start.1
  258.7 1.4 copy-start.3
Sparse Core Ops, SparseCore 0:
  10.1 52.6 all-gather.1
  264.0 66.5 reduce-scatter.1

commit v9 on v8

--- a/solution.py
+++ b/solution.py
@@ -124,12 +124,12 @@
         * slot_dots[:, None, :],
         axis=2,
     )
-    reduced = lax.psum_scatter(
-        jnp.stack([combined_part, input_part]).astype(jnp.bfloat16).reshape(2, tok_rows, -1),
-        BLOCK_AXES,
-        scatter_dimension=2,
-        tiled=True,
+    block_count = full_width // width_share
+    to_reduce = jnp.stack([combined_part, input_part]).astype(jnp.bfloat16)
+    reduced_blocks = lax.all_to_all(
+        to_reduce.reshape(2, tok_rows, block_count, width_share), BLOCK_AXES, 2, 2, tiled=True
     )
+    reduced = jnp.sum(reduced_blocks.astype(jnp.float32), axis=2).astype(jnp.bfloat16)
     gate_grad = lax.psum(partial_dots, BLOCK_AXES)
     combined = reduced[0]
     input_grad = reduced[1]

time: 343 us -> 355 us (1.035)
  blocking collectives: 110 us -> 147 us
  waiting for transfers between devices: 153 us -> 118 us
  starting transfers between devices: 8.91 us -> 16.6 us
    psum x1, blocking collectives: 31.4 us -> 68 us  [per_device(): gate_grad = lax.psum(partial_dots, BLOCK_AXES)]
    reduce_scatter x1 -> x0, waiting for transfers between devices: 35.3 us -> none  [per_device(): lax.psum_scatter(jnp.stack([combined_part, input_part]).astype(jnp.bfloat...]
    all_to_all x0 -> x1, starting transfers between devices: none -> 7.76 us  [per_device(): lax.all_to_all(to_reduce.reshape(2, tok_rows, block_count, width_share),...]
    unnamed x19 -> x21, local copies, waits for them, and re-layouts: 9.04 us -> 8.21 us
  transfers between devices with their start and end apart: 3 -> 3, of which waited for: 3 -> 2; matrix products, arithmetic and copies ran while one was open for 2% -> 2% of each run, Pallas kernels for 0% -> 0%
where the time goes in v9:
time: 355 us; the launch traced here: 354 us
  blocking collectives  147 us (41%)
  waiting for transfers between devices  118 us (33%)
  local copies, waits for them, and re-layouts  33.9 us (10%)
  matrix products  17.2 us (5%)
  starting transfers between devices  16.6 us (5%)
  between operations  14.2 us (4%)
  other arithmetic  7.22 us (2%)
    all_to_all x1, blocking collectives, per_device(): lax.all_to_all(send_parts, 'expert', split_axis=0, concat_axis=0, tiled=T...  78.7 us
    all_to_all x1, waiting for transfers between devices, per_device(): lax.all_to_all(send_xg, 'expert', split_axis=0, concat_axis=0, tiled=True)  69.2 us
    psum x1, blocking collectives, per_device(): gate_grad = lax.psum(partial_dots, BLOCK_AXES)  68 us
    all_gather x1, waiting for transfers between devices, per_device(): whole_stacked = lax.all_gather(stacked, BLOCK_AXES, axis=2, tiled=True)  48.9 us
    all_to_all x1, starting transfers between devices, per_device(): lax.all_to_all(send_xg, 'expert', split_axis=0, concat_axis=0, tiled=True)  8.83 us
    unnamed x21, local copies, waits for them, and re-layouts  8.21 us
    all_to_all x1, starting transfers between devices, per_device(): lax.all_to_all(to_reduce.reshape(2, tok_rows, block_count, width_share),...  7.76 us
  transfers between devices with their start and end apart: 3, of which 2 were waited for; matrix products, arithmetic and copies ran while one was open for 2% of the time, Pallas kernels for 0%

profile of v9, /device:TPU:1, one launch (start us, length us, event | category | flops | bytes accessed | tf_op | source)
XLA Modules:
  0.0 354.0 jit_solution(13922733648187909395)
XLA Ops:
  7.2 0.0 copy-start
  7.2 0.0 all-gather.2.cloned.1.call-start
  7.2 1.1 copy.123
  8.3 1.0 copy.124
  9.3 0.7 pad_maximum_fusion.3
  9.9 0.0 all-gather.2.cloned.1.call-update
  10.0 0.8 copy.119
  10.8 0.1 eq.45
  10.9 0.1 eq.49
  11.1 0.6 reduce-window.6
  11.7 0.2 slice_reduce_fusion
  11.9 0.1 fusion.74
  12.0 0.1 reduce_sum.54
  12.2 0.1 copy.122
  12.2 0.8 copy.128
  13.0 0.1 mul.108
  13.2 0.7 multiply_add_fusion.2
  13.9 0.1 fusion.67
  14.0 48.9 %all-gather.2.cloned.1.call-done = bf16[128,2,2048]{0,2,1:T(8,128)(2,1)} async-done(((bf16[128,2,256]{0,2,1:T(8,128)(2,1)}), bf16[128,2,2048]{0,2,1:T(8,128)(2,1)}) %all-gather.2.cloned.1.call-update) | async-done | bytes 1048592 | tf_op jit(solution)/shard_map/all_gather | solution.py:65
  62.8 1.3 fusion.90
  64.1 0.6 convolution_convert_fusion.1
  64.7 2.2 copy.127
  66.9 1.2 copy.129
  68.1 1.9 mul.110
  70.0 0.7 convolution_convert_fusion.2
  70.7 0.0 copy-start.2
  70.7 1.0 copy.130
  71.8 0.4 copy-done.2
  72.1 2.1 pad_maximum_fusion
  74.2 8.8 %all-to-all-start = ((bf16[64,192,128]{2,1,0:T(8,128)(2,1)}), bf16[64,192,128]{2,1,0:T(8,128)(2,1)}, u32[]{:S(2)}, u32[]{:S(2)}) async-start(bf16[64,192,128]{2,1,0:T(8,128)(2,1)} %pad_maximum_fusion), calls=%async_computation | async-start | bytes 6291456 | tf_op jit(solution)/shard_map/all_to_all | solution.py:77
  83.0 3.6 %copy.149 = bf16[64,8,16,128]{3,2,1,0:T(8,128)(2,1)} copy(bf16[64,8,16,128]{3,1,2,0:T(8,128)(2,1)} %bitcast.105) | data formatting | bytes 4194304
  86.6 69.2 %all-to-all-done = bf16[64,192,128]{2,1,0:T(8,128)(2,1)} async-done(((bf16[64,192,128]{2,1,0:T(8,128)(2,1)}), bf16[64,192,128]{2,1,0:T(8,128)(2,1)}, u32[]{:S(2)}, u32[]{:S(2)}) %all-to-all-start) | async-done | bytes 3145760 | tf_op jit(solution)/shard_map/all_to_all | solution.py:77
  155.8 3.2 fusion.89
  159.1 0.0 copy-done
  159.1 1.0 fusion.10
  160.0 0.0 copy-start.7
  160.1 0.6 copy-done.4
  160.7 2.3 fusion.4
  163.0 0.0 copy-done.7
  163.0 5.6 %convolution_convert_fusion = bf16[384,16,128]{2,0,1:T(8,128)(2,1)} fusion(bf16[16,128,512]{2,1,0:T(8,128)(2,1)S(1)} %bitcast.89, bf16[512,16,128]{2,1,0:T(8,128)(2,1)} %bitcast.106, bf16[384,16,128]{2,1,0:T(8,128)(2,1)} %bitcast.109, f32[384,512]{1,0:T(8,128)} %copy-done.7), kind=kOutput, calls=%fused_computation.8 | convolution fusion | flops 1615134720 | bytes 8126464 | tf_op jit(solution)/shard_map/dot_general | solution.py:94
  168.6 2.5 copy.133
  171.1 0.0 copy-done.5
  171.1 1.0 copy.136
  172.2 0.4 pad_maximum_fusion.1
  172.6 78.7 %all_to_all.15 = bf16[64,192,128]{2,1,0:T(8,128)(2,1)S(1)} all-to-all(bf16[64,192,128]{2,1,0:T(8,128)(2,1)S(1)} %pad_maximum_fusion.1), channel_id=1, replica_groups=mesh['sec'=2,'section'=4,'expert'=64] {'expert'}, dimensions={0} | all-to-all | bytes 6291456 | tf_op jit(solution)/shard_map/all_to_all | solution.py:101
  251.3 1.9 fusion.88
  253.2 2.8 copy.137
  256.0 2.0 convolution_bitcast_fusion
  258.0 0.0 copy-done.6
  258.0 0.2 fusion.54
  258.2 0.0 copy-done.1
  258.3 0.6 fusion.69
  258.8 1.6 fusion.77
  260.4 2.9 copy.139
  263.2 2.9 fusion.28
  266.1 1.0 add_convert_fusion
  267.1 1.2 copy.140
  268.4 1.1 pad_maximum_fusion.2
  269.5 1.1 copy.141
  270.6 7.8 %all-to-all-start.2 = ((bf16[2,128,8,256]{3,1,0,2:T(8,128)(2,1)}), bf16[2,128,8,256]{3,1,0,2:T(8,128)(2,1)S(1)}, u32[]{:S(2)}, u32[]{:S(2)}) async-start(bf16[2,128,8,256]{3,1,0,2:T(8,128)(2,1)} %copy.141), calls=%async_computation.2 | async-start | bytes 2097152 | tf_op jit(solution)/shard_map/all_to_all | solution.py:129
  278.3 68.0 %psum.7 = f32[128,2]{0,1:T(2,128)} all-reduce(f32[128,2]{0,1:T(2,128)S(1)} %get-tuple-element.3), channel_id=1, replica_groups=mesh['sec'=2,'section'=4,'expert'=64] {'sec','section'}, use_global_device_ids=true, to_apply=%region_7.8 | all-reduce | flops 256 | bytes 2048 | tf_op jit(solution)/shard_map/psum | solution.py:133
  346.4 0.0 all-to-all-done.2
  346.4 0.1 reduce_sum.57
  346.5 0.7 slice_bitcast_fusion
  (10 shorter events, 0.1 us)
Async XLA Ops:
  7.2 151.9 %copy-start = (bf16[1,2048,512]{2,1,0:T(8,128)(2,1)S(1)}, bf16[1,2048,512]{2,1,0:T(8,128)(2,1)}, u32[]{:S(2)}) copy-start(bf16[1,2048,512]{2,1,0:T(8,128)(2,1)} %param.10) | copy-start | bytes 6291460
  7.2 55.7 %all-gather.2.cloned.1.call-start = ((), (), s32[]{:S(2)}) async-start(), calls=%async_computation.3 | async-start | bytes 1179648 | tf_op jit(solution)/shard_map/all_gather | solution.py:65
  70.7 1.4 copy-start.2
  74.2 81.6 %all-to-all-start = ((bf16[64,192,128]{2,1,0:T(8,128)(2,1)}), bf16[64,192,128]{2,1,0:T(8,128)(2,1)}, u32[]{:S(2)}, u32[]{:S(2)}) async-start(bf16[64,192,128]{2,1,0:T(8,128)(2,1)} %pad_maximum_fusion), calls=%async_computation | async-start | bytes 6291456 | tf_op jit(solution)/shard_map/all_to_all | solution.py:77
  159.1 1.6 copy-start.4
  160.0 2.9 copy-start.7
  168.6 2.5 copy-start.5
  256.0 2.0 copy-start.6
  256.0 2.2 copy-start.1
  263.2 2.9 copy-start.3
  270.6 75.8 %all-to-all-start.2 = ((bf16[2,128,8,256]{3,1,0,2:T(8,128)(2,1)}), bf16[2,128,8,256]{3,1,0,2:T(8,128)(2,1)S(1)}, u32[]{:S(2)}, u32[]{:S(2)}) async-start(bf16[2,128,8,256]{3,1,0,2:T(8,128)(2,1)} %copy.141), calls=%async_computation.2 | async-start | bytes 2097152 | tf_op jit(solution)/shard_map/all_to_all | solution.py:129
Sparse Core Ops, SparseCore 0:
  10.1 52.6 all-gather.1

commit v10 on v8

--- a/solution.py
+++ b/solution.py
@@ -65,11 +65,12 @@
     whole_stacked = lax.all_gather(stacked, BLOCK_AXES, axis=2, tiled=True)
     whole_tokens = whole_stacked[:, 0, :].reshape(tok_rows, groups, lane)
     whole_cot = whole_stacked[:, 1, :].reshape(tok_rows, groups, lane)
-    whole_grad = (
-        gate_values[:, :, None, None] * whole_cot[:, None, :, :].astype(jnp.float32)
-    ).astype(jnp.bfloat16)
+    gate_slot = jnp.sum(
+        jnp.where(pair_to_slot > 0, gate_values.reshape(-1)[:, None], 0.0), axis=0
+    )
     send_x = gather_rows(token_to_slot, whole_tokens)
-    send_g = gather_rows(pair_to_slot, whole_grad.reshape(2 * tok_rows, groups, lane))
+    cot_slot = gather_rows(token_to_slot, whole_cot)
+    send_g = (gate_slot[:, None, None] * cot_slot.astype(jnp.float32)).astype(jnp.bfloat16)
     send_xg = jnp.concatenate(
         [send_x.reshape(experts, chunk_rows, lane), send_g.reshape(experts, chunk_rows, lane)],
         axis=1,

time: 343 us -> 338 us (0.985)
  local copies, waits for them, and re-layouts: 30.6 us -> 26 us
    unnamed x19 -> x17, local copies, waits for them, and re-layouts: 9.04 us -> 8.66 us
where the time goes in v10:
time: 338 us; the launch traced here: 333 us
  waiting for transfers between devices  153 us (45%)
  blocking collectives  110 us (33%)
  local copies, waits for them, and re-layouts  26 us (8%)
  matrix products  14.4 us (4%)
  between operations  14.2 us (4%)
  starting transfers between devices  8.91 us (3%)
  other arithmetic  7.38 us (2%)
    all_to_all x1, blocking collectives, per_device(): lax.all_to_all(send_parts, 'expert', split_axis=0, concat_axis=0, tiled=T...  78.7 us
    all_to_all x1, waiting for transfers between devices, per_device(): lax.all_to_all(send_xg, 'expert', split_axis=0, concat_axis=0, tiled=True)  69.2 us
    all_gather x1, waiting for transfers between devices, per_device(): whole_stacked = lax.all_gather(stacked, BLOCK_AXES, axis=2, tiled=True)  48.7 us
    reduce_scatter x1, waiting for transfers between devices, per_device(): lax.psum_scatter(jnp.stack([combined_part, input_part]).astype(jnp.bfloat...  34.7 us
    psum x1, blocking collectives, per_device(): gate_grad = lax.psum(partial_dots, BLOCK_AXES)  31.2 us
    unnamed x17, local copies, waits for them, and re-layouts  8.66 us
    all_to_all x1, starting transfers between devices, per_device(): lax.all_to_all(send_xg, 'expert', split_axis=0, concat_axis=0, tiled=True)  8.65 us
  transfers between devices with their start and end apart: 3, of which 3 were waited for; matrix products, arithmetic and copies ran while one was open for 2% of the time, Pallas kernels for 0%

profile of v10, /device:TPU:1, one launch (start us, length us, event | category | flops | bytes accessed | tf_op | source)
XLA Modules:
  0.0 333.5 jit_solution(6010565937613052486)
XLA Ops:
  7.2 0.0 copy-start
  7.2 0.0 all-gather.2.cloned.1.call-start
  7.2 1.1 copy.91
  8.3 1.0 copy.92
  9.3 0.7 pad_maximum_fusion.3
  9.9 0.0 all-gather.2.cloned.1.call-update
  10.0 0.8 copy.87
  10.8 0.1 eq.45
  10.9 0.1 eq.49
  11.1 0.6 reduce-window.6
  11.7 0.2 slice_reduce_fusion
  11.9 0.1 fusion.73
  12.0 0.1 reduce_sum.51
  12.2 0.1 copy.90
  12.2 0.8 copy.96
  13.0 0.1 broadcast_in_dim.20
  13.2 0.7 multiply_add_fusion.2
  13.9 0.1 fusion.67
  14.0 0.1 select_reduce_fusion
  14.1 48.7 %all-gather.2.cloned.1.call-done = bf16[128,2,2048]{0,2,1:T(8,128)(2,1)} async-done(((bf16[128,2,256]{0,2,1:T(8,128)(2,1)}), bf16[128,2,2048]{0,2,1:T(8,128)(2,1)}) %all-gather.2.cloned.1.call-update) | async-done | bytes 1048592 | tf_op jit(solution)/shard_map/all_gather | solution.py:65
  62.8 1.3 fusion.89
  64.1 0.6 convolution_convert_fusion.3
  64.7 1.0 copy.95
  65.8 0.6 multiply_convert_fusion
  66.4 1.0 copy.99
  67.4 2.1 pad_maximum_fusion
  69.5 8.6 %all-to-all-start = ((bf16[64,192,128]{2,1,0:T(8,128)(2,1)}), bf16[64,192,128]{2,1,0:T(8,128)(2,1)}, u32[]{:S(2)}, u32[]{:S(2)}) async-start(bf16[64,192,128]{2,1,0:T(8,128)(2,1)} %pad_maximum_fusion), calls=%async_computation | async-start | bytes 6291456 | tf_op jit(solution)/shard_map/all_to_all | solution.py:78
  78.2 0.2 reduce-scatter.2.cloned.1.call-start
  78.4 3.6 %copy.119 = bf16[64,8,16,128]{3,2,1,0:T(8,128)(2,1)} copy(bf16[64,8,16,128]{3,1,2,0:T(8,128)(2,1)} %bitcast.105) | data formatting | bytes 4194304
  82.0 69.2 %all-to-all-done = bf16[64,192,128]{2,1,0:T(8,128)(2,1)} async-done(((bf16[64,192,128]{2,1,0:T(8,128)(2,1)}), bf16[64,192,128]{2,1,0:T(8,128)(2,1)}, u32[]{:S(2)}, u32[]{:S(2)}) %all-to-all-start) | async-done | bytes 3145760 | tf_op jit(solution)/shard_map/all_to_all | solution.py:78
  151.1 3.2 fusion.88
  154.3 0.0 copy-done
  154.3 0.0 copy-start.3
  154.3 1.0 fusion.13
  155.3 0.6 copy-done.3
  155.9 2.3 fusion.5
  158.2 5.5 %convolution_convert_fusion.1 = bf16[384,16,128]{2,0,1:T(8,128)(2,1)} fusion(bf16[16,128,512]{2,1,0:T(8,128)(2,1)S(1)} %bitcast.91, bf16[512,16,128]{2,1,0:T(8,128)(2,1)} %bitcast.106, bf16[384,16,128]{2,1,0:T(8,128)(2,1)} %bitcast.109, f32[384,512]{1,0:T(8,128)S(1)} %fusion.13), kind=kOutput, calls=%fused_computation.10 | convolution fusion | flops 1615134720 | bytes 8126464 | tf_op jit(solution)/shard_map/dot_general | solution.py:95
  163.7 0.0 copy-start.4
  163.7 2.5 copy.102
  166.2 0.0 copy-done.4
  166.3 1.0 copy.105
  167.3 0.4 pad_maximum_fusion.1
  167.7 78.7 %all_to_all.10 = bf16[64,192,128]{2,1,0:T(8,128)(2,1)S(1)} all-to-all(bf16[64,192,128]{2,1,0:T(8,128)(2,1)S(1)} %pad_maximum_fusion.1), channel_id=1, replica_groups=mesh['sec'=2,'section'=4,'expert'=64] {'expert'}, dimensions={0} | all-to-all | bytes 6291456 | tf_op jit(solution)/shard_map/all_to_all | solution.py:102
  246.4 1.9 fusion.87
  248.3 2.8 copy.106
  251.1 0.0 copy-start.5
  251.1 0.0 copy-start.1
  251.1 2.0 convolution_bitcast_fusion
  253.1 0.0 copy-done.5
  253.1 0.2 fusion.55
  253.4 0.0 copy-done.1
  253.4 0.6 fusion.68
  253.9 0.0 copy-start.2
  253.9 0.6 fusion.76
  254.5 0.8 copy-done.2
  255.3 1.3 fusion
  256.6 0.1 add_convert_fusion
  256.8 0.2 copy.108
  257.0 2.1 pad_maximum_fusion.2
  259.1 0.0 reduce-scatter.2.cloned.1.call-update
  259.1 31.2 %psum.7 = f32[128,2]{0,1:T(2,128)} all-reduce(f32[128,2]{0,1:T(2,128)S(1)} %get-tuple-element.3), channel_id=1, replica_groups=mesh['sec'=2,'section'=4,'expert'=64] {'sec','section'}, use_global_device_ids=true, to_apply=%region_8.9 | all-reduce | flops 256 | bytes 2048 | tf_op jit(solution)/shard_map/psum | solution.py:134
  290.4 34.7 %reduce-scatter.2.cloned.1.call-done = bf16[2,128,256]{2,1,0:T(8,128)(2,1)} async-done(((bf16[2,128,2048]{2,1,0:T(8,128)(2,1)}), bf16[2,128,256]{2,1,0:T(8,128)(2,1)}) %reduce-scatter.2.cloned.1.call-update) | async-done | bytes 131088 | tf_op jit(solution)/shard_map/reduce_scatter | solution.py:128
  325.1 1.5 slice_bitcast_fusion
  (4 shorter events, 0.1 us)
Async XLA Ops:
  7.2 147.2 %copy-start = (bf16[1,2048,512]{2,1,0:T(8,128)(2,1)S(1)}, bf16[1,2048,512]{2,1,0:T(8,128)(2,1)}, u32[]{:S(2)}) copy-start(bf16[1,2048,512]{2,1,0:T(8,128)(2,1)} %param.10) | copy-start | bytes 6291460
  7.2 55.7 %all-gather.2.cloned.1.call-start = ((), (), s32[]{:S(2)}) async-start(), calls=%async_computation.3 | async-start | bytes 1179648 | tf_op jit(solution)/shard_map/all_gather | solution.py:65
  69.5 81.6 %all-to-all-start = ((bf16[64,192,128]{2,1,0:T(8,128)(2,1)}), bf16[64,192,128]{2,1,0:T(8,128)(2,1)}, u32[]{:S(2)}, u32[]{:S(2)}) async-start(bf16[64,192,128]{2,1,0:T(8,128)(2,1)} %pad_maximum_fusion), calls=%async_computation | async-start | bytes 6291456 | tf_op jit(solution)/shard_map/all_to_all | solution.py:78
  78.2 246.9 %reduce-scatter.2.cloned.1.call-start = ((), (), s32[]{:S(2)}) async-start(), calls=%async_computation.4 | async-start | bytes 1179648 | tf_op jit(solution)/shard_map/reduce_scatter | solution.py:128
  154.3 1.6 copy-start.3
  163.7 2.5 copy-start.4
  251.1 2.0 copy-start.5
  251.1 2.2 copy-start.1
  253.9 1.4 copy-start.2
Sparse Core Ops, SparseCore 0:
  10.1 52.6 all-gather.1
  259.2 65.7 reduce-scatter.1

commit v11 on v10

--- a/solution.py
+++ b/solution.py
@@ -63,21 +63,24 @@
 
     stacked = jnp.stack([tokens, cotangent], axis=1)
     whole_stacked = lax.all_gather(stacked, BLOCK_AXES, axis=2, tiled=True)
-    whole_tokens = whole_stacked[:, 0, :].reshape(tok_rows, groups, lane)
     whole_cot = whole_stacked[:, 1, :].reshape(tok_rows, groups, lane)
     gate_slot = jnp.sum(
         jnp.where(pair_to_slot > 0, gate_values.reshape(-1)[:, None], 0.0), axis=0
     )
-    send_x = gather_rows(token_to_slot, whole_tokens)
-    cot_slot = gather_rows(token_to_slot, whole_cot)
-    send_g = (gate_slot[:, None, None] * cot_slot.astype(jnp.float32)).astype(jnp.bfloat16)
-    send_xg = jnp.concatenate(
-        [send_x.reshape(experts, chunk_rows, lane), send_g.reshape(experts, chunk_rows, lane)],
-        axis=1,
+    stream_scale = jnp.stack([jnp.ones_like(gate_slot), gate_slot], axis=1)
+    slot_rows = lax.dot_general(
+        token_to_slot,
+        whole_stacked.reshape(tok_rows, 2, groups, lane),
+        (((0,), (0,)), ((), ())),
+        preferred_element_type=jnp.float32,
     )
-    recv_xg = lax.all_to_all(send_xg, "expert", split_axis=0, concat_axis=0, tiled=True)
-    recv_x = recv_xg[:, :chunk_rows].reshape(slot_count, groups, lane)
-    recv_g = recv_xg[:, chunk_rows:].reshape(slot_count, groups, lane)
+    send_xg = (stream_scale[:, :, None, None] * slot_rows).astype(jnp.bfloat16)
+    recv_xg = lax.all_to_all(
+        send_xg.reshape(experts, 2 * chunk_rows, lane), "expert", split_axis=0, concat_axis=0,
+        tiled=True,
+    ).reshape(slot_count, 2, groups, lane)
+    recv_x = recv_xg[:, 0]
+    recv_g = recv_xg[:, 1]
     expand_3d = expand_local.reshape(groups, lane, -1)
     contract_3d = contract_local.reshape(-1, groups, lane)
     hidden = lax.dot_general(

time: 338 us -> 342 us (1.012)
  blocking collectives: 110 us -> 31.2 us
  waiting for transfers between devices: 153 us -> 226 us
  starting transfers between devices: 8.91 us -> 15 us
    all_to_all x1 -> x0, blocking collectives: 78.7 us -> none  [per_device(): lax.all_to_all(send_parts, 'expert', split_axis=0, concat_axis=0, tiled=T...]
    all_to_all x1 -> x2, waiting for transfers between devices: 69.2 us -> 141 us  [the longest x1 71.6 us: per_device(): lax.all_to_all(send_parts, 'expert', split_axis=0, concat_axis=0, tiled=T...]
    all_to_all x1 -> x2, starting transfers between devices: 8.65 us -> 14.9 us  [the longest x1 8.83 us: per_device(): lax.all_to_all(send_xg.reshape(experts, 2 * chunk_rows, lane), 'expert',...]
    unnamed x17 -> x19, local copies, waits for them, and re-layouts: 8.66 us -> 7.84 us
  transfers between devices with their start and end apart: 3 -> 4, of which waited for: 3 -> 4; matrix products, arithmetic and copies ran while one was open for 2% -> 3% of each run, Pallas kernels for 0% -> 0%
where the time goes in v11:
time: 342 us; the launch traced here: 338 us
  waiting for transfers between devices  226 us (66%)
  blocking collectives  31.2 us (9%)
  local copies, waits for them, and re-layouts  28.8 us (8%)
  matrix products  16.2 us (5%)
  starting transfers between devices  15 us (4%)
  between operations  14.2 us (4%)
  other arithmetic  5.88 us (2%)
    all_to_all x1, waiting for transfers between devices, per_device(): lax.all_to_all(send_parts, 'expert', split_axis=0, concat_axis=0, tiled=T...  71.6 us
    all_to_all x1, waiting for transfers between devices, per_device(): lax.all_to_all(send_xg.reshape(experts, 2 * chunk_rows, lane), 'expert',...  69.2 us
    all_gather x1, waiting for transfers between devices, per_device(): whole_stacked = lax.all_gather(stacked, BLOCK_AXES, axis=2, tiled=True)  48.7 us
    reduce_scatter x1, waiting for transfers between devices, per_device(): lax.psum_scatter(jnp.stack([combined_part, input_part]).astype(jnp.bfloat...  36.8 us
    psum x1, blocking collectives, per_device(): gate_grad = lax.psum(partial_dots, BLOCK_AXES)  31.2 us
    all_to_all x1, starting transfers between devices, per_device(): lax.all_to_all(send_xg.reshape(experts, 2 * chunk_rows, lane), 'expert',...  8.83 us
    unnamed x19, local copies, waits for them, and re-layouts  7.84 us
  transfers between devices with their start and end apart: 4, of which 4 were waited for; matrix products, arithmetic and copies ran while one was open for 3% of the time, Pallas kernels for 0%

profile of v11, /device:TPU:1, one launch (start us, length us, event | category | flops | bytes accessed | tf_op | source)
XLA Modules:
  0.0 337.7 jit_solution(8459619603048969754)
XLA Ops:
  7.2 0.0 copy-start
  7.2 0.0 all-gather.2.cloned.1.call-start
  7.2 1.1 copy.62
  8.3 1.0 copy.63
  9.3 0.7 pad_maximum_fusion.2
  9.9 0.0 all-gather.2.cloned.1.call-update
  10.0 0.8 copy.57
  10.8 0.1 eq.49
  10.9 0.1 eq.45
  11.0 0.6 reduce-window.6
  11.7 0.2 slice_reduce_fusion
  11.9 0.1 fusion.58
  12.0 0.1 reduce_sum.51
  12.1 0.1 copy.60
  12.2 0.8 copy.61
  13.0 0.1 broadcast_in_dim.20
  13.2 0.1 select_reduce_fusion
  13.3 0.7 multiply_add_fusion.2
  14.0 0.1 fusion.53
  14.1 48.7 %all-gather.2.cloned.1.call-done = bf16[128,2,2048]{0,2,1:T(8,128)(2,1)} async-done(((bf16[128,2,256]{0,2,1:T(8,128)(2,1)}), bf16[128,2,2048]{0,2,1:T(8,128)(2,1)}) %all-gather.2.cloned.1.call-update) | async-done | bytes 1048592 | tf_op jit(solution)/shard_map/all_gather | solution.py:65
  62.8 2.5 multiply_convert_fusion
  65.3 3.7 %copy.66 = bf16[384,2,16,128]{3,2,1,0:T(8,128)(2,1)} copy(bf16[384,2,16,128]{3,0,2,1:T(8,128)(2,1)S(1)} %multiply_convert_fusion) | data formatting | bytes 6291456 | tf_op jit(solution)/shard_map/convert_element_type | solution.py:77
  69.0 8.8 %all-to-all-start = ((bf16[64,192,128]{2,1,0:T(8,128)(2,1)}), bf16[64,192,128]{2,1,0:T(8,128)(2,1)}, u32[]{:S(2)}, u32[]{:S(2)}) async-start(bf16[64,192,128]{2,1,0:T(8,128)(2,1)} %bitcast.106), calls=%async_computation | async-start | bytes 6291456 | tf_op jit(solution)/shard_map/all_to_all | solution.py:78
  77.9 3.6 %copy.85 = bf16[64,8,16,128]{3,2,1,0:T(8,128)(2,1)} copy(bf16[64,8,16,128]{3,1,2,0:T(8,128)(2,1)} %bitcast.115) | data formatting | bytes 4194304
  81.5 69.2 %all-to-all-done = bf16[64,192,128]{2,1,0:T(8,128)(2,1)} async-done(((bf16[64,192,128]{2,1,0:T(8,128)(2,1)}), bf16[64,192,128]{2,1,0:T(8,128)(2,1)}, u32[]{:S(2)}, u32[]{:S(2)}) %all-to-all-start) | async-done | bytes 3145760 | tf_op jit(solution)/shard_map/all_to_all | solution.py:78
  150.7 3.6 %fusion.73 = (bf16[384,1,16,128]{3,2,1,0:T(8,128)(2,1)S(1)}, bf16[384,1,16,128]{3,2,1,0:T(8,128)(2,1)}) fusion(bf16[384,2,16,128]{3,2,1,0:T(8,128)(2,1)} %bitcast.6), kind=kLoop, calls=%fused_computation.87 | loop fusion | bytes 6291456 | tf_op jit(solution)/shard_map/slice | solution.py:82
  154.2 0.0 copy-done
  154.2 0.0 copy-start.3
  154.2 1.0 fusion.11
  155.2 0.6 copy-done.3
  155.8 2.3 fusion.5
  158.1 5.4 %convolution_convert_fusion.1 = bf16[384,16,128]{2,0,1:T(8,128)(2,1)} fusion(bf16[16,128,512]{2,1,0:T(8,128)(2,1)S(1)} %bitcast.103, bf16[512,16,128]{2,1,0:T(8,128)(2,1)} %bitcast.116, bf16[384,1,16,128]{3,2,1,0:T(8,128)(2,1)} %get-tuple-element.8, f32[384,512]{1,0:T(8,128)S(1)} %fusion.11), kind=kOutput, calls=%fused_computation.9 | convolution fusion | flops 1615134720 | bytes 8126464 | tf_op jit(solution)/shard_map/dot_general | solution.py:98
  163.6 0.0 copy-start.5
  163.6 2.5 copy.72
  166.1 0.0 copy-done.5
  166.1 1.0 copy.69
  167.1 2.1 pad_maximum_fusion
  169.2 0.0 copy-start.2
  169.2 6.1 %all-to-all-start.1 = ((bf16[64,192,128]{2,1,0:T(8,128)(2,1)}), bf16[64,192,128]{2,1,0:T(8,128)(2,1)}, u32[]{:S(2)}, u32[]{:S(2)}) async-start(bf16[64,192,128]{2,1,0:T(8,128)(2,1)} %pad_maximum_fusion), calls=%async_computation.1 | async-start | bytes 6291456 | tf_op jit(solution)/shard_map/all_to_all | solution.py:105
  175.3 0.0 reduce-scatter.2.cloned.1.call-start
  175.4 0.0 copy-done.2
  175.4 0.8 slice.43
  176.2 71.6 %all-to-all-done.1 = bf16[64,192,128]{2,1,0:T(8,128)(2,1)} async-done(((bf16[64,192,128]{2,1,0:T(8,128)(2,1)}), bf16[64,192,128]{2,1,0:T(8,128)(2,1)}, u32[]{:S(2)}, u32[]{:S(2)}) %all-to-all-start.1) | async-done | bytes 3145760 | tf_op jit(solution)/shard_map/all_to_all | solution.py:105
  247.8 3.8 %fusion.72 = (bf16[64,96,128]{2,1,0:T(8,128)(2,1)}, bf16[64,96,128]{2,1,0:T(8,128)(2,1)}) fusion(bf16[64,192,128]{2,1,0:T(8,128)(2,1)} %all-to-all-done.1), kind=kLoop, calls=%fused_computation.86 | loop fusion | bytes 6291456 | tf_op jit(solution)/shard_map/slice | solution.py:106
  251.6 0.0 copy-start.4
  251.6 2.9 copy.73
  254.6 0.0 copy-start.6
  254.6 0.0 copy-start.1
  254.6 0.0 copy-done.4
  254.6 2.0 convolution_bitcast_fusion
  256.6 0.0 copy-done.6
  256.6 0.2 fusion.41
  256.8 0.0 copy-done.1
  256.8 0.6 fusion.54
  257.4 0.6 fusion.61
  258.0 0.1 add_convert_fusion
  258.1 0.2 copy.75
  258.3 1.9 fusion
  260.2 1.1 pad_maximum_fusion.1
  261.3 0.0 reduce-scatter.2.cloned.1.call-update
  261.3 31.2 %psum.7 = f32[128,2]{0,1:T(2,128)} all-reduce(f32[128,2]{0,1:T(2,128)S(1)} %get-tuple-element.3), channel_id=1, replica_groups=mesh['sec'=2,'section'=4,'expert'=64] {'sec','section'}, use_global_device_ids=true, to_apply=%region_8.9 | all-reduce | flops 256 | bytes 2048 | tf_op jit(solution)/shard_map/psum | solution.py:137
  292.5 36.8 %reduce-scatter.2.cloned.1.call-done = bf16[2,128,256]{2,1,0:T(8,128)(2,1)} async-done(((bf16[2,128,2048]{2,1,0:T(8,128)(2,1)}), bf16[2,128,256]{2,1,0:T(8,128)(2,1)}) %reduce-scatter.2.cloned.1.call-update) | async-done | bytes 131088 | tf_op jit(solution)/shard_map/reduce_scatter | solution.py:131
  329.3 1.5 slice_bitcast_fusion
  (6 shorter events, 0.1 us)
Async XLA Ops:
  7.2 147.1 %copy-start = (bf16[1,2048,512]{2,1,0:T(8,128)(2,1)S(1)}, bf16[1,2048,512]{2,1,0:T(8,128)(2,1)}, u32[]{:S(2)}) copy-start(bf16[1,2048,512]{2,1,0:T(8,128)(2,1)} %param.10) | copy-start | bytes 6291460
  7.2 55.7 %all-gather.2.cloned.1.call-start = ((), (), s32[]{:S(2)}) async-start(), calls=%async_computation.3 | async-start | bytes 1179648 | tf_op jit(solution)/shard_map/all_gather | solution.py:65
  69.0 81.6 %all-to-all-start = ((bf16[64,192,128]{2,1,0:T(8,128)(2,1)}), bf16[64,192,128]{2,1,0:T(8,128)(2,1)}, u32[]{:S(2)}, u32[]{:S(2)}) async-start(bf16[64,192,128]{2,1,0:T(8,128)(2,1)} %bitcast.106), calls=%async_computation | async-start | bytes 6291456 | tf_op jit(solution)/shard_map/all_to_all | solution.py:78
  154.2 1.6 copy-start.3
  163.6 2.5 copy-start.5
  169.2 6.1 %copy-start.2 = (bf16[128,2,2048]{0,2,1:T(8,128)(2,1)S(1)}, bf16[128,2,2048]{0,2,1:T(8,128)(2,1)}, u32[]{:S(2)}) copy-start(bf16[128,2,2048]{0,2,1:T(8,128)(2,1)} %all-gather.2.cloned.1.call-done) | copy-start | bytes 3145732
  169.2 78.6 %all-to-all-start.1 = ((bf16[64,192,128]{2,1,0:T(8,128)(2,1)}), bf16[64,192,128]{2,1,0:T(8,128)(2,1)}, u32[]{:S(2)}, u32[]{:S(2)}) async-start(bf16[64,192,128]{2,1,0:T(8,128)(2,1)} %pad_maximum_fusion), calls=%async_computation.1 | async-start | bytes 6291456 | tf_op jit(solution)/shard_map/all_to_all | solution.py:105
  175.3 154.0 %reduce-scatter.2.cloned.1.call-start = ((), (), s32[]{:S(2)}) async-start(), calls=%async_computation.4 | async-start | bytes 1179648 | tf_op jit(solution)/shard_map/reduce_scatter | solution.py:131
  251.6 2.9 copy-start.4
  254.6 2.0 copy-start.6
  254.6 2.3 copy-start.1
Sparse Core Ops, SparseCore 0:
  10.1 52.6 all-gather.1
  261.4 67.8 reduce-scatter.1
